TPU v7x, 32 devices: a whole 2x2x4 slice. The times are simulated.
32 devices in a mesh: ax: 2 (over y), az: 16 (over z, x, core).
Axes of the slice: x: 2, y: 2, z: 4, core: 2. Of those that a mesh axis runs over, the one named last changes fastest.
Arguments:
- state: float32 [4, 64, 128, 128], P(None, 'ax', 'az'), may hold values from -6 to 6
- final_adjoint: float32 [4, 64, 128, 128], P(None, 'ax', 'az'), may hold values from -6 to 6
- resistance: float32 [512], replicated, may hold values from 0.2 to 2
- wall_patch: int32 [64, 128], P('ax', 'az'), may hold values from 0 to 511
- patch_slot_index: int32 [512], replicated, may hold values from 0 to 1023, as said below
Outputs:
- initial_adjoint: float32 [4, 64, 128, 128], P(None, 'ax', 'az')
- patch_gradient: float32 [1024], P('az')
Inputs may be any that keep to these rules, and one draw needn't show every extreme that they name: `patch_slot_index`: the values are distinct; 0 and 1023 are always among them.
All inputs are finite; a program needn't handle non-finite values.
Results may differ from a plain program's by a relative error of at most 0.0003.
Values sent between devices are 32-bit elements; how exact they have to be, the bound alone decides.
No kernel may reach another device: no remote copies, remote signals or barrier semaphores. Data moves between devices by JAX's collectives and lax.ppermute only.
A program may use at most 128 MiB of HBM per device.

v0:
```python
import functools

import jax
import jax.numpy as jnp
from jax import lax
from jax.experimental import pallas as pl
from jax.experimental.pallas import tpu as pltpu
from jax.sharding import PartitionSpec as P

ITERS = 4


mach_number = 0.5
time_step = 0.3


def steps_kernel(
    axial_local, azim_local, radial_count, width, axial_total,
    axis_ref, state_ref, adjoint_ref, liner_ref, axial_lo_ref, axial_hi_ref, azim_ref,
    out_ref, grad_ref,
    field_a, field_b, adj_a, adj_b, liner_pad, walls,
):
    rows = axial_local + 2 * width
    cols = azim_local + 2 * width
    own = slice(width, width + axial_local)
    own_cols = slice(0, azim_local)

    for buf, lo in ((field_a, 0), (adj_a, 4)):
        buf[:, own, own_cols] = state_ref[...] if lo == 0 else adjoint_ref[...]
        buf[:, 0:width, own_cols] = axial_lo_ref[lo : lo + 4]
        buf[:, width + axial_local : rows, own_cols] = axial_hi_ref[lo : lo + 4]
        buf[:, :, azim_local:cols] = azim_ref[lo : lo + 4]
    liner_pad[own, own_cols] = liner_ref[...]
    liner_pad[0:width, own_cols] = axial_lo_ref[8]
    liner_pad[width + axial_local : rows, own_cols] = axial_hi_ref[8]
    liner_pad[:, azim_local:cols] = azim_ref[8]

    first_row = axis_ref[0] * axial_local - width
    lane = lax.broadcasted_iota(jnp.int32, (cols, radial_count), 1)
    not_last = lane != radial_count - 1
    not_first = lane != 0

    def radial_diff(x):
        upper = jnp.where(not_last, pltpu.roll(x, radial_count - 1, 1), 0.0)
        lower = jnp.where(not_first, pltpu.roll(x, 1, 1), 0.0)
        return (upper - lower) * 0.5

    def azim_diff(x):
        return (pltpu.roll(x, cols - 1, 0) - pltpu.roll(x, 1, 0)) * 0.5

    def advance(src, dst, step, orient):
        def body(r, carry):
            centre = src[:, r]
            along = (src[:, r + 1] - src[:, r - 1]) * 0.5
            press, axial, azim, radial = centre[0], centre[1], centre[2], centre[3]
            rate_press = (
                orient * (-mach_number * along[0] - along[1] - azim_diff(azim) - radial_diff(radial))
                - liner_pad[r] * press
            )
            rate_axial = orient * (-mach_number * along[1] - along[0])
            rate_azim = orient * (-mach_number * along[2] - azim_diff(press))
            rate_radial = orient * (-mach_number * along[3] - radial_diff(press))
            g = first_row + r
            keep = jnp.where((g >= 0) & (g < axial_total), 1.0, 0.0)
            dst[0, r] = (press + time_step * rate_press) * keep
            dst[1, r] = (axial + time_step * rate_axial) * keep
            dst[2, r] = (azim + time_step * rate_azim) * keep
            dst[3, r] = (radial + time_step * rate_radial) * keep
            return carry

        lax.fori_loop(step, rows - step, body, 0)

    walls[0] = state_ref[0]
    bufs = (field_a, field_b)
    for step in range(1, ITERS):
        advance(bufs[(step - 1) % 2], bufs[step % 2], step, 1.0)
        walls[step] = bufs[step % 2][0, own, own_cols]

    grad_ref[...] = jnp.zeros(grad_ref.shape, jnp.float32)
    bufs = (adj_a, adj_b)
    for step in range(1, ITERS + 1):
        grad_ref[...] = grad_ref[...] - time_step * bufs[(step - 1) % 2][0, own, own_cols] * walls[ITERS - step]
        advance(bufs[(step - 1) % 2], bufs[step % 2], step, -1.0)
    out_ref[...] = bufs[ITERS % 2][:, own, own_cols]


def shards(state, final_adjoint, resistance, wall_patch, patch_slot_index):
    width = ITERS
    axial_local = state.shape[1]
    azim_local = state.shape[2]
    radial_count = state.shape[3]
    wall = (jnp.arange(radial_count) == radial_count - 1).astype(jnp.float32)
    liner = resistance[wall_patch][:, :, None] * wall[None, None, :]

    def pack(sl_axis, start, stop):
        parts = [lax.slice_in_dim(x, start, stop, axis=sl_axis) for x in (state, final_adjoint)]
        parts.append(lax.slice_in_dim(liner, start, stop, axis=sl_axis - 1)[None])
        return jnp.concatenate(parts, axis=0)

    ax_count = lax.axis_size("ax")
    az_count = lax.axis_size("az")
    axial_lo, axial_hi = lax.ppermute(
        pack(1, axial_local - width, axial_local), "ax", [(i, i + 1) for i in range(ax_count - 1)]
    ), lax.ppermute(pack(1, 0, width), "ax", [(i + 1, i) for i in range(ax_count - 1)])

    def azim_pack(start, stop):
        return jnp.concatenate(
            [axial_lo[:, :, start:stop], pack(2, start, stop), axial_hi[:, :, start:stop]], axis=1
        )

    azim_prev = lax.ppermute(
        azim_pack(azim_local - width, azim_local), "az", [(i, (i + 1) % az_count) for i in range(az_count)]
    )
    azim_next = lax.ppermute(azim_pack(0, width), "az", [((i + 1) % az_count, i) for i in range(az_count)])
    azim_halo = jnp.concatenate([azim_next, azim_prev], axis=2)

    rows = axial_local + 2 * width
    cols = azim_local + 2 * width
    axis_index = jnp.reshape(lax.axis_index("ax"), (1,)).astype(jnp.int32)
    kernel = functools.partial(
        steps_kernel, axial_local, azim_local, radial_count, width, axial_local * ax_count
    )
    vmem = pl.BlockSpec(memory_space=pltpu.VMEM)
    adjoint, grad = pl.pallas_call(
        kernel,
        out_shape=(
            jax.ShapeDtypeStruct(state.shape, jnp.float32),
            jax.ShapeDtypeStruct((axial_local, azim_local, radial_count), jnp.float32),
        ),
        in_specs=[pl.BlockSpec(memory_space=pltpu.SMEM)] + [vmem] * 6,
        out_specs=(vmem, vmem),
        scratch_shapes=[pltpu.VMEM((4, rows, cols, radial_count), jnp.float32)] * 4
        + [
            pltpu.VMEM((rows, cols, radial_count), jnp.float32),
            pltpu.VMEM((ITERS, axial_local, azim_local, radial_count), jnp.float32),
        ],
    )(axis_index, state, final_adjoint, liner, axial_lo, axial_hi, azim_halo)
    cell_grad = grad[:, :, radial_count - 1]

    slot_total = 2 * resistance.shape[0]
    cell_slot = patch_slot_index[wall_patch].reshape(-1)
    onehot = (cell_slot[:, None] == jnp.arange(slot_total, dtype=jnp.int32)[None, :]).astype(jnp.float32)
    slot_vector = jnp.dot(cell_grad.reshape(-1), onehot, precision=lax.Precision.HIGHEST)
    total = lax.psum(slot_vector, ("ax", "az"))
    owned = slot_total // az_count
    patch_gradient = lax.dynamic_slice_in_dim(total, lax.axis_index("az") * owned, owned)
    return (adjoint, patch_gradient)


def solution(mesh):
    return jax.shard_map(
        shards,
        mesh=mesh,
        in_specs=(P(None, "ax", "az", None), P(None, "ax", "az", None), P(), P("ax", "az"), P()),
        out_specs=(P(None, "ax", "az", None), P("az")),
        check_vma=False,
    )
```

profile of v0, /device:TPU:0, one launch (start us, length us, event | category | flops | bytes accessed | tf_op | source)
XLA Modules:
  0.0 101.6 jit_solution(1387247197728652056)
XLA Ops:
  0.6 0.0 copy-start
  0.7 0.7 compare_select_fusion
  1.3 0.1 copy.7
  1.4 0.1 reshape.17
  1.5 0.0 copy-done
  1.5 0.0 copy-start.2
  1.6 0.0 copy-start.3
  1.6 1.9 %gather_fusion = f32[256]{0:T(256)S(1)} fusion(f32[512]{0:T(512)S(1)} %copy-done, s32[1024]{0:T(1024)S(1)} %pad_clamp_fusion), kind=kCustom, calls=%fused_computation | custom fusion | bytes 3072 | tf_op jit(solution)/shard_map/gather | solution.py:93
  3.5 0.1 reshape.16
  3.6 0.1 broadcast_multiply_fusion.liner_ref
  3.7 0.0 copy-start.4
  3.7 0.0 copy-done.2
  3.7 0.0 copy-done.3
  3.8 4.9 %collective-permute-start = (f32[9,4,8,128]{3,2,1,0:T(8,128)S(1)}, f32[9,4,8,128]{3,2,1,0:T(8,128)S(1)}, u32[]{:S(2)}, u32[]{:S(2)}) collective-permute-start(f32[9,4,8,128]{3,2,1,0:T(8,128)S(1)} %pad_maximum_fusion.3), channel_id=1, source_target_pairs={{0,16},{1,17},{2,18},{3,19},{4,20},{5,21},{6,22},{7,23},{8,24},{9,... | collective-permute-start | bytes 442376 | tf_op jit(solution)/shard_map/ppermute | solution.py:102
  8.7 1.3 %collective-permute-start.1 = (f32[9,4,8,128]{3,2,1,0:T(8,128)S(1)}, f32[9,4,8,128]{3,2,1,0:T(8,128)S(1)}, u32[]{:S(2)}, u32[]{:S(2)}) collective-permute-start(f32[9,4,8,128]{3,2,1,0:T(8,128)S(1)} %pad_maximum_fusion.4), channel_id=1, source_target_pairs={{16,0},{17,1},{18,2},{19,3},{20,4},{21,5},{22,6},{23,7},{24,8},{25... | collective-permute-start | bytes 442376 | tf_op jit(solution)/shard_map/ppermute | solution.py:104
  10.0 0.2 fusion.2
  10.2 0.0 copy-done.4
  10.2 1.5 %collective-permute-done.axial_lo_ref = f32[9,4,8,128]{3,2,1,0:T(8,128)S(1)} collective-permute-done((f32[9,4,8,128]{3,2,1,0:T(8,128)S(1)}, f32[9,4,8,128]{3,2,1,0:T(8,128)S(1)}, u32[]{:S(2)}, u32[]{:S(2)}) %collective-permute-start) | collective-permute-done | bytes 147488 | tf_op jit(solution)/shard_map/ppermute | solution.py:102
  11.8 0.0 copy-start.5
  11.8 4.1 %collective-permute-done.1.axial_hi_ref = f32[9,4,8,128]{3,2,1,0:T(8,128)S(1)} collective-permute-done((f32[9,4,8,128]{3,2,1,0:T(8,128)S(1)}, f32[9,4,8,128]{3,2,1,0:T(8,128)S(1)}, u32[]{:S(2)}, u32[]{:S(2)}) %collective-permute-start.1) | collective-permute-done | bytes 147488 | tf_op jit(solution)/shard_map/ppermute | solution.py:104
  15.9 0.0 copy-start.6
  15.9 0.0 copy-start.1
  16.0 0.2 pad_maximum_fusion.2
  16.1 0.1 collective-permute-start.3
  16.2 0.2 pad_maximum_fusion.1
  16.4 0.0 copy-done.5
  16.4 0.2 copy-done.6
  16.6 4.3 %collective-permute-start.2 = (f32[9,40,4,128]{3,2,1,0:T(4,128)S(1)}, f32[9,40,4,128]{3,2,1,0:T(4,128)S(1)}, u32[]{:S(2)}, u32[]{:S(2)}) collective-permute-start(f32[9,40,4,128]{3,2,1,0:T(4,128)S(1)} %pad_maximum_fusion.1), channel_id=1, source_target_pairs={{1,0},{2,1},{3,2},{4,3},{5,4},{6,5},{7,6},{8,7},{9,8},{10,9},{11,1... | collective-permute-start | bytes 2211848 | tf_op jit(solution)/shard_map/ppermute | solution.py:114
  20.9 0.0 copy-done.1
  20.9 1.9 %gather_fusion.1 = s32[256]{0:T(256)S(1)} fusion(s32[512]{0:T(512)S(1)} %copy-done.1, s32[1024]{0:T(1024)S(1)} %pad_clamp_fusion), kind=kCustom, calls=%fused_computation.1 | custom fusion | bytes 3072 | tf_op jit(solution)/shard_map/gather | solution.py:141
  22.9 7.0 %collective-permute-done.3 = f32[9,40,4,128]{3,2,1,0:T(4,128)S(1)} collective-permute-done((f32[9,40,4,128]{3,2,1,0:T(4,128)S(1)}, f32[9,40,4,128]{3,2,1,0:T(4,128)S(1)}, u32[]{:S(2)}, u32[]{:S(2)}) %collective-permute-start.3) | collective-permute-done | bytes 737312 | tf_op jit(solution)/shard_map/ppermute | solution.py:111
  29.9 0.0 collective-permute-done.2
  29.9 1.4 %pad_maximum_fusion.azim_ref = f32[9,40,8,128]{3,2,1,0:T(8,128)} fusion(f32[9,40,4,128]{3,2,1,0:T(4,128)S(1)} %collective-permute-done.3, f32[9,40,4,128]{3,2,1,0:T(4,128)S(1)} %collective-permute-done.2), kind=kLoop, calls=%fused_computation.2 | loop fusion | flops 368640 | bytes 2949120 | tf_op jit(solution)/shard_map/concatenate | solution.py:115
  31.3 23.9 %shard_map.68 = (f32[4,32,8,128]{3,2,1,0:T(8,128)}, f32[32,8,128]{2,1,0:T(8,128)}) custom-call(s32[1]{0:T(128)} %bitcast.axis_ref, f32[4,32,8,128]{3,2,1,0:T(8,128)} %state_ref.1, f32[4,32,8,128]{3,2,1,0:T(8,128)} %adjoint_ref.1, f32[32,8,128]{2,1,0:T(8,128)} %copy-done.4, f32[9,4,8,128]{3,2,1,0:T(8,128)} %copy-done.5, f32[9,4,8,128]{3,2,1,0:T(8,128)} %copy-done.6, ...), custom_call_target="tpu_custom_call" | custom-call | tf_op jit(solution)/shard_map/pallas_call | solution.py:124
  55.2 1.1 %slice_reduce_fusion = f32[32,8]{1,0:T(8,128)S(1)} fusion(f32[32,8,128]{2,1,0:T(8,128)} %get-tuple-element.5), kind=kLoop, calls=%fused_computation.10 | loop fusion | bytes 2048 | tf_op jit(solution)/shard_map/slice | solution.py:138
  56.3 0.1 reshape.36
  56.4 0.5 fusion
  56.9 44.1 %psum.7 = f32[1024]{0:T(1024)S(1)} all-reduce(f32[1024]{0:T(1024)S(1)} %bitcast.11), channel_id=1, replica_groups=mesh['ax'=2,'az'=16] {'ax','az'}, use_global_device_ids=true, to_apply=%region_0.0 | all-reduce | flops 1024 | bytes 8192 | tf_op jit(solution)/shard_map/psum | solution.py:144
  101.0 0.6 dynamic_slice.3
  (9 shorter events, 0.1 us)
Async XLA Ops:
  0.6 0.9 copy-start
  1.5 2.2 %copy-start.2 = (f32[4,32,8,128]{3,2,1,0:T(8,128)S(1)}, f32[4,32,8,128]{3,2,1,0:T(8,128)}, u32[]{:S(2)}) copy-start(f32[4,32,8,128]{3,2,1,0:T(8,128)} %state_ref.1) | copy-start | bytes 1572868
  1.6 2.2 %copy-start.3 = (f32[4,32,8,128]{3,2,1,0:T(8,128)S(1)}, f32[4,32,8,128]{3,2,1,0:T(8,128)}, u32[]{:S(2)}) copy-start(f32[4,32,8,128]{3,2,1,0:T(8,128)} %adjoint_ref.1) | copy-start | bytes 1572868
  3.7 6.5 %copy-start.4 = (f32[32,8,128]{2,1,0:T(8,128)}, f32[32,8,128]{2,1,0:T(8,128)S(1)}, u32[]{:S(2)}) copy-start(f32[32,8,128]{2,1,0:T(8,128)S(1)} %broadcast_multiply_fusion.liner_ref) | copy-start | bytes 393220
  3.8 8.0 %collective-permute-start = (f32[9,4,8,128]{3,2,1,0:T(8,128)S(1)}, f32[9,4,8,128]{3,2,1,0:T(8,128)S(1)}, u32[]{:S(2)}, u32[]{:S(2)}) collective-permute-start(f32[9,4,8,128]{3,2,1,0:T(8,128)S(1)} %pad_maximum_fusion.3), channel_id=1, source_target_pairs={{0,16},{1,17},{2,18},{3,19},{4,20},{5,21},{6,22},{7,23},{8,24},{9,... | collective-permute-start | bytes 442376 | tf_op jit(solution)/shard_map/ppermute | solution.py:102
  8.7 7.2 %collective-permute-start.1 = (f32[9,4,8,128]{3,2,1,0:T(8,128)S(1)}, f32[9,4,8,128]{3,2,1,0:T(8,128)S(1)}, u32[]{:S(2)}, u32[]{:S(2)}) collective-permute-start(f32[9,4,8,128]{3,2,1,0:T(8,128)S(1)} %pad_maximum_fusion.4), channel_id=1, source_target_pairs={{16,0},{17,1},{18,2},{19,3},{20,4},{21,5},{22,6},{23,7},{24,8},{25... | collective-permute-start | bytes 442376 | tf_op jit(solution)/shard_map/ppermute | solution.py:104
  11.8 4.6 %copy-start.5 = (f32[9,4,8,128]{3,2,1,0:T(8,128)}, f32[9,4,8,128]{3,2,1,0:T(8,128)S(1)}, u32[]{:S(2)}) copy-start(f32[9,4,8,128]{3,2,1,0:T(8,128)S(1)} %collective-permute-done.axial_lo_ref) | copy-start | bytes 442372
  15.9 0.7 copy-start.6
  15.9 5.0 %copy-start.1 = (s32[512]{0:T(512)S(1)}, s32[512]{0:T(512)}, u32[]{:S(2)}) copy-start(s32[512]{0:T(512)} %param.9) | copy-start | bytes 6148
  16.1 13.7 %collective-permute-start.3 = (f32[9,40,4,128]{3,2,1,0:T(4,128)S(1)}, f32[9,40,4,128]{3,2,1,0:T(4,128)S(1)}, u32[]{:S(2)}, u32[]{:S(2)}) collective-permute-start(f32[9,40,4,128]{3,2,1,0:T(4,128)S(1)} %pad_maximum_fusion.2), channel_id=1, source_target_pairs={{0,1},{1,2},{2,3},{3,4},{4,5},{5,6},{6,7},{7,8},{8,9},{9,10},{10,1... | collective-permute-start | bytes 2211848 | tf_op jit(solution)/shard_map/ppermute | solution.py:111
  16.6 13.3 %collective-permute-start.2 = (f32[9,40,4,128]{3,2,1,0:T(4,128)S(1)}, f32[9,40,4,128]{3,2,1,0:T(4,128)S(1)}, u32[]{:S(2)}, u32[]{:S(2)}) collective-permute-start(f32[9,40,4,128]{3,2,1,0:T(4,128)S(1)} %pad_maximum_fusion.1), channel_id=1, source_target_pairs={{1,0},{2,1},{3,2},{4,3},{5,4},{6,5},{7,6},{8,7},{9,8},{10,9},{11,1... | collective-permute-start | bytes 2211848 | tf_op jit(solution)/shard_map/ppermute | solution.py:114
where the time goes:
time: 102 us
  blocking collectives  44.1 us (43%)
  Pallas kernels  23.9 us (23%)
  waiting for transfers between devices  12.7 us (12%)
  starting transfers between devices  10.6 us (10%)
  local copies, waits for them, and re-layouts  6.36 us (6%)
  other arithmetic  2.63 us (3%)
    psum x1, blocking collectives, shards(): total = lax.psum(slot_vector, ('ax', 'az'))  44.1 us
    pallas_call x1, Pallas kernels, shards(): pl.pallas_call(kernel, out_shape=(jax.ShapeDtypeStruct(state.shape, jnp.f...  23.9 us
    ppermute x1, waiting for transfers between devices, shards(): lax.ppermute(azim_pack(azim_local - width, azim_local), 'az', [(i, (i + 1...  7.03 us
    ppermute x1, starting transfers between devices, shards(): lax.ppermute(pack(1, axial_local - width, axial_local), 'ax', [(i, i + 1)...  4.88 us
    ppermute x1, starting transfers between devices, shards(): lax.ppermute(azim_pack(0, width), 'az', [((i + 1) % az_count, i) for i in...  4.33 us
    ppermute x1, waiting for transfers between devices, shards(): lax.ppermute(pack(1, 0, width), 'ax', [(i + 1, i) for i in range(ax_count...  4.11 us
  transfers between devices with their start and end apart: 4, of which 3 were waited for; matrix products, arithmetic and copies ran while one was open for 2% of the time, Pallas kernels for 0%

commit v1 on v0

--- a/solution.py
+++ b/solution.py
@@ -90,7 +90,10 @@
     azim_local = state.shape[2]
     radial_count = state.shape[3]
     wall = (jnp.arange(radial_count) == radial_count - 1).astype(jnp.float32)
-    liner = resistance[wall_patch][:, :, None] * wall[None, None, :]
+    patch_count = resistance.shape[0]
+    patch_onehot = (wall_patch[:, :, None] == jnp.arange(patch_count, dtype=jnp.int32)).astype(jnp.float32)
+    damping = jnp.dot(patch_onehot, resistance, precision=lax.Precision.HIGHEST)
+    liner = damping[:, :, None] * wall[None, None, :]
 
     def pack(sl_axis, start, stop):
         parts = [lax.slice_in_dim(x, start, stop, axis=sl_axis) for x in (state, final_adjoint)]
@@ -141,9 +144,9 @@
     cell_slot = patch_slot_index[wall_patch].reshape(-1)
     onehot = (cell_slot[:, None] == jnp.arange(slot_total, dtype=jnp.int32)[None, :]).astype(jnp.float32)
     slot_vector = jnp.dot(cell_grad.reshape(-1), onehot, precision=lax.Precision.HIGHEST)
-    total = lax.psum(slot_vector, ("ax", "az"))
     owned = slot_total // az_count
-    patch_gradient = lax.dynamic_slice_in_dim(total, lax.axis_index("az") * owned, owned)
+    send = jnp.tile(slot_vector.reshape(az_count, owned), (ax_count, 1))
+    patch_gradient = lax.all_to_all(send, ("ax", "az"), 0, 0, tiled=True).sum(0)
     return (adjoint, patch_gradient)
 
 

time: 102 us -> 76.1 us (0.75)
  blocking collectives: 44.1 us -> 16.3 us
  matrix products: 0.5 us -> 2.68 us
  waiting for transfers between devices: 12.7 us -> 14.3 us
    psum x1 -> x0, blocking collectives: 44.1 us -> none  [shards(): total = lax.psum(slot_vector, ('ax', 'az'))]
    all_to_all x0 -> x1, blocking collectives: none -> 16.3 us  [shards(): patch_gradient = lax.all_to_all(send, ('ax', 'az'), 0, 0, tiled=True).sum(0)]
    ppermute x1, waiting for transfers between devices: 0.01 us -> 6.52 us  [shards(): lax.ppermute(azim_pack(0, width), 'az', [((i + 1) % az_count, i) for i in...]
    ppermute x1, waiting for transfers between devices: 4.11 us -> 1.63 us  [shards(): lax.ppermute(pack(1, 0, width), 'ax', [(i + 1, i) for i in range(ax_count...]
    ppermute x1, waiting for transfers between devices: 7.03 us -> 4.97 us  [shards(): lax.ppermute(azim_pack(azim_local - width, azim_local), 'az', [(i, (i + 1...]
    gather x2 -> x0, local copies, waits for them, and re-layouts: 2.02 us -> none  [shards(): liner = resistance[wall_patch][:, :, None] * wall[None, None, :]]
    dot_general x0 -> x1, matrix products: none -> 1.9 us  [shards(): damping = jnp.dot(patch_onehot, resistance, precision=lax.Precision.HIGHEST)]
  transfers between devices with their start and end apart: 4 -> 4, of which waited for: 3 -> 4; matrix products, arithmetic and copies ran while one was open for 2% -> 3% of each run, Pallas kernels for 0% -> 0%
where the time goes in v1:
time: 76.1 us; the launch traced here: 75.8 us
  Pallas kernels  23.9 us (31%)
  blocking collectives  16.3 us (21%)
  waiting for transfers between devices  14.3 us (19%)
  starting transfers between devices  9.8 us (13%)
  local copies, waits for them, and re-layouts  5.43 us (7%)
  matrix products  2.68 us (4%)
  other arithmetic  2.51 us (3%)
  between operations  0.89 us (1%)
    pallas_call x1, Pallas kernels, shards(): pl.pallas_call(kernel, out_shape=(jax.ShapeDtypeStruct(state.shape, jnp.f...  23.9 us
    all_to_all x1, blocking collectives, shards(): patch_gradient = lax.all_to_all(send, ('ax', 'az'), 0, 0, tiled=True).sum(0)  16.3 us
    ppermute x1, waiting for transfers between devices, shards(): lax.ppermute(azim_pack(0, width), 'az', [((i + 1) % az_count, i) for i in...  6.52 us
    ppermute x1, waiting for transfers between devices, shards(): lax.ppermute(azim_pack(azim_local - width, azim_local), 'az', [(i, (i + 1...  4.97 us
    ppermute x1, starting transfers between devices, shards(): lax.ppermute(pack(1, axial_local - width, axial_local), 'ax', [(i, i + 1)...  4.89 us
    ppermute x1, starting transfers between devices, shards(): lax.ppermute(azim_pack(0, width), 'az', [((i + 1) % az_count, i) for i in...  3.57 us
    gather x1, local copies, waits for them, and re-layouts, shards(): cell_slot = patch_slot_index[wall_patch].reshape(-1)  1.95 us
    dot_general x1, matrix products, shards(): damping = jnp.dot(patch_onehot, resistance, precision=lax.Precision.HIGHEST)  1.9 us
  transfers between devices with their start and end apart: 4, of which 4 were waited for; matrix products, arithmetic and copies ran while one was open for 3% of the time, Pallas kernels for 0%

profile of v1, /device:TPU:0, one launch (start us, length us, event | category | flops | bytes accessed | tf_op | source)
XLA Modules:
  0.0 75.8 jit_solution(4459763542920739886)
XLA Ops:
  0.6 0.0 copy-start
  0.6 0.0 copy-start.2
  0.7 0.0 copy-start.3
  0.7 0.8 %copy.10 = s32[32,8]{1,0:T(8,128)S(1)} copy(s32[32,8]{0,1:T(8,128)} %param.8) | data formatting | bytes 2048 | tf_op args[3]
  1.5 0.0 copy-done
  1.5 1.9 %fusion.4 = f32[1,32,8]{2,0,1:T(1,128)S(1)} fusion(f32[512,1,1]{0,1,2:T(1,128)S(1)} %bitcast.17, s32[32,8]{1,0:T(8,128)S(1)} %copy.10), kind=kOutput, calls=%fused_computation.9 | convolution fusion | flops 1703936 | bytes 4096 | tf_op jit(solution)/shard_map/dot_general | solution.py:95
  3.4 0.1 broadcast_multiply_fusion.liner_ref
  3.5 0.0 copy-start.4
  3.6 1.0 %fusion.8 = (f32[4,4,8,128]{3,2,1,0:T(8,128)S(1)}, f32[4,4,8,128]{3,2,1,0:T(8,128)S(1)}, f32[4,4,8,128]{3,2,1,0:T(8,128)S(1)}, f32[4,4,8,128]{3,2,1,0:T(8,128)S(1)}) fusion(f32[4,32,8,128]{3,2,1,0:T(8,128)} %state_ref.1, f32[4,32,8,128]{3,2,1,0:T(8,128)} %adjoint_ref.1), kind=kLoop, calls=%fused_computation.25 | loop fusion | bytes 524288 | tf_op jit(solution)/shard_map/slice | solution.py:99
  4.6 1.3 %collective-permute-start.1 = (f32[9,4,8,128]{3,2,1,0:T(8,128)S(1)}, f32[9,4,8,128]{3,2,1,0:T(8,128)S(1)}, u32[]{:S(2)}, u32[]{:S(2)}) collective-permute-start(f32[9,4,8,128]{3,2,1,0:T(8,128)S(1)} %pad_maximum_fusion.4), channel_id=1, source_target_pairs={{16,0},{17,1},{18,2},{19,3},{20,4},{21,5},{22,6},{23,7},{24,8},{25... | collective-permute-start | bytes 442376 | tf_op jit(solution)/shard_map/ppermute | solution.py:107
  5.9 4.9 %collective-permute-start = (f32[9,4,8,128]{3,2,1,0:T(8,128)S(1)}, f32[9,4,8,128]{3,2,1,0:T(8,128)S(1)}, u32[]{:S(2)}, u32[]{:S(2)}) collective-permute-start(f32[9,4,8,128]{3,2,1,0:T(8,128)S(1)} %pad_maximum_fusion.3), channel_id=1, source_target_pairs={{0,16},{1,17},{2,18},{3,19},{4,20},{5,21},{6,22},{7,23},{8,24},{9,... | collective-permute-start | bytes 442376 | tf_op jit(solution)/shard_map/ppermute | solution.py:105
  10.8 0.0 copy-done.2
  10.8 0.0 copy-done.3
  10.8 0.2 fusion.6
  11.0 0.0 copy-done.4
  11.1 1.6 %collective-permute-done.1.axial_hi_ref = f32[9,4,8,128]{3,2,1,0:T(8,128)S(1)} collective-permute-done((f32[9,4,8,128]{3,2,1,0:T(8,128)S(1)}, f32[9,4,8,128]{3,2,1,0:T(8,128)S(1)}, u32[]{:S(2)}, u32[]{:S(2)}) %collective-permute-start.1) | collective-permute-done | bytes 147488 | tf_op jit(solution)/shard_map/ppermute | solution.py:107
  12.7 0.0 copy-start.5
  12.7 1.2 %collective-permute-done.axial_lo_ref = f32[9,4,8,128]{3,2,1,0:T(8,128)S(1)} collective-permute-done((f32[9,4,8,128]{3,2,1,0:T(8,128)S(1)}, f32[9,4,8,128]{3,2,1,0:T(8,128)S(1)}, u32[]{:S(2)}, u32[]{:S(2)}) %collective-permute-start) | collective-permute-done | bytes 147488 | tf_op jit(solution)/shard_map/ppermute | solution.py:105
  13.9 0.0 copy-start.6
  13.9 0.0 copy-start.7
  13.9 0.0 copy-start.1
  13.9 0.2 pad_maximum_fusion.1
  14.1 3.6 %collective-permute-start.2 = (f32[9,40,4,128]{3,2,1,0:T(4,128)S(1)}, f32[9,40,4,128]{3,2,1,0:T(4,128)S(1)}, u32[]{:S(2)}, u32[]{:S(2)}) collective-permute-start(f32[9,40,4,128]{3,2,1,0:T(4,128)S(1)} %pad_maximum_fusion.1), channel_id=1, source_target_pairs={{1,0},{2,1},{3,2},{4,3},{5,4},{6,5},{7,6},{8,7},{9,8},{10,9},{11,1... | collective-permute-start | bytes 2211848 | tf_op jit(solution)/shard_map/ppermute | solution.py:117
  17.7 0.2 pad_maximum_fusion.2
  17.9 0.0 copy-done.5
  17.9 0.0 copy-done.6
  17.9 0.1 collective-permute-start.3
  18.0 0.0 copy-done.7
  18.0 0.1 copy.11
  18.1 0.1 reshape.46
  18.2 0.0 copy-done.1
  18.2 1.9 %gather_fusion = s32[256]{0:T(256)S(1)} fusion(s32[512]{0:T(512)S(1)} %copy-done.1, s32[1024]{0:T(1024)S(1)} %pad_clamp_fusion), kind=kCustom, calls=%fused_computation | custom fusion | bytes 3072 | tf_op jit(solution)/shard_map/gather | solution.py:144
  20.2 6.5 %collective-permute-done.2 = f32[9,40,4,128]{3,2,1,0:T(4,128)S(1)} collective-permute-done((f32[9,40,4,128]{3,2,1,0:T(4,128)S(1)}, f32[9,40,4,128]{3,2,1,0:T(4,128)S(1)}, u32[]{:S(2)}, u32[]{:S(2)}) %collective-permute-start.2) | collective-permute-done | bytes 737312 | tf_op jit(solution)/shard_map/ppermute | solution.py:117
  26.7 5.0 %collective-permute-done.3 = f32[9,40,4,128]{3,2,1,0:T(4,128)S(1)} collective-permute-done((f32[9,40,4,128]{3,2,1,0:T(4,128)S(1)}, f32[9,40,4,128]{3,2,1,0:T(4,128)S(1)}, u32[]{:S(2)}, u32[]{:S(2)}) %collective-permute-start.3) | collective-permute-done | bytes 737312 | tf_op jit(solution)/shard_map/ppermute | solution.py:114
  31.7 1.4 %pad_maximum_fusion.azim_ref = f32[9,40,8,128]{3,2,1,0:T(8,128)} fusion(f32[9,40,4,128]{3,2,1,0:T(4,128)S(1)} %collective-permute-done.3, f32[9,40,4,128]{3,2,1,0:T(4,128)S(1)} %collective-permute-done.2), kind=kLoop, calls=%fused_computation.1 | loop fusion | flops 368640 | bytes 2949120 | tf_op jit(solution)/shard_map/concatenate | solution.py:118
  33.1 23.9 %shard_map.68 = (f32[4,32,8,128]{3,2,1,0:T(8,128)}, f32[32,8,128]{2,1,0:T(8,128)}) custom-call(s32[1]{0:T(128)} %bitcast.axis_ref, f32[4,32,8,128]{3,2,1,0:T(8,128)} %state_ref.1, f32[4,32,8,128]{3,2,1,0:T(8,128)} %adjoint_ref.1, f32[32,8,128]{2,1,0:T(8,128)} %copy-done.4, f32[9,4,8,128]{3,2,1,0:T(8,128)} %copy-done.6, f32[9,4,8,128]{3,2,1,0:T(8,128)} %copy-done.5, ...), custom_call_target="tpu_custom_call" | custom-call | tf_op jit(solution)/shard_map/pallas_call | solution.py:127
  57.0 1.1 %slice_reduce_fusion = f32[32,8]{1,0:T(8,128)S(1)} fusion(f32[32,8,128]{2,1,0:T(8,128)} %get-tuple-element.5), kind=kLoop, calls=%fused_computation.13 | loop fusion | bytes 2048 | tf_op jit(solution)/shard_map/slice | solution.py:141
  58.1 0.1 reshape.57
  58.1 0.8 %fusion = f32[1,16,64]{2,0,1:T(1,128)S(1)} fusion(f32[256,1,1]{0,1,2:T(1,128)S(1)} %reshape.57, s32[256]{0:T(256)S(1)} %gather_fusion, s32[16,64]{1,0:T(8,128)S(1)} %multiply_add_fusion), kind=kOutput, calls=%fused_computation.2 | convolution fusion | flops 3407872 | bytes 10240 | tf_op jit(solution)/shard_map/dot_general | solution.py:146
  58.9 16.3 %all_to_all.9 = f32[32,1,64]{2,1,0:T(1,128)S(1)} all-to-all(f32[32,1,64]{2,1,0:T(1,128)S(1)} %bitcast.18), channel_id=1, replica_groups=mesh['ax'=2,'az'=16] {'ax','az'}, dimensions={0} | all-to-all | bytes 16384 | tf_op jit(solution)/shard_map/all_to_all | solution.py:149
  75.2 0.6 reduce_sum.9
  (11 shorter events, 0.1 us)
Async XLA Ops:
  0.6 0.9 %copy-start = (f32[512]{0:T(512)S(1)}, f32[512]{0:T(512)}, u32[]{:S(2)}) copy-start(f32[512]{0:T(512)} %param.7) | copy-start | bytes 6148
  0.6 10.2 %copy-start.2 = (f32[4,32,8,128]{3,2,1,0:T(8,128)S(1)}, f32[4,32,8,128]{3,2,1,0:T(8,128)}, u32[]{:S(2)}) copy-start(f32[4,32,8,128]{3,2,1,0:T(8,128)} %state_ref.1) | copy-start | bytes 1572868
  0.7 10.2 %copy-start.3 = (f32[4,32,8,128]{3,2,1,0:T(8,128)S(1)}, f32[4,32,8,128]{3,2,1,0:T(8,128)}, u32[]{:S(2)}) copy-start(f32[4,32,8,128]{3,2,1,0:T(8,128)} %adjoint_ref.1) | copy-start | bytes 1572868
  3.5 7.5 %copy-start.4 = (f32[32,8,128]{2,1,0:T(8,128)}, f32[32,8,128]{2,1,0:T(8,128)S(1)}, u32[]{:S(2)}) copy-start(f32[32,8,128]{2,1,0:T(8,128)S(1)} %broadcast_multiply_fusion.liner_ref) | copy-start | bytes 393220
  4.6 8.1 %collective-permute-start.1 = (f32[9,4,8,128]{3,2,1,0:T(8,128)S(1)}, f32[9,4,8,128]{3,2,1,0:T(8,128)S(1)}, u32[]{:S(2)}, u32[]{:S(2)}) collective-permute-start(f32[9,4,8,128]{3,2,1,0:T(8,128)S(1)} %pad_maximum_fusion.4), channel_id=1, source_target_pairs={{16,0},{17,1},{18,2},{19,3},{20,4},{21,5},{22,6},{23,7},{24,8},{25... | collective-permute-start | bytes 442376 | tf_op jit(solution)/shard_map/ppermute | solution.py:107
  5.9 8.0 %collective-permute-start = (f32[9,4,8,128]{3,2,1,0:T(8,128)S(1)}, f32[9,4,8,128]{3,2,1,0:T(8,128)S(1)}, u32[]{:S(2)}, u32[]{:S(2)}) collective-permute-start(f32[9,4,8,128]{3,2,1,0:T(8,128)S(1)} %pad_maximum_fusion.3), channel_id=1, source_target_pairs={{0,16},{1,17},{2,18},{3,19},{4,20},{5,21},{6,22},{7,23},{8,24},{9,... | collective-permute-start | bytes 442376 | tf_op jit(solution)/shard_map/ppermute | solution.py:105
  12.7 5.2 %copy-start.5 = (f32[9,4,8,128]{3,2,1,0:T(8,128)}, f32[9,4,8,128]{3,2,1,0:T(8,128)S(1)}, u32[]{:S(2)}) copy-start(f32[9,4,8,128]{3,2,1,0:T(8,128)S(1)} %collective-permute-done.1.axial_hi_ref) | copy-start | bytes 442372
  13.9 4.0 %copy-start.6 = (f32[9,4,8,128]{3,2,1,0:T(8,128)}, f32[9,4,8,128]{3,2,1,0:T(8,128)S(1)}, u32[]{:S(2)}) copy-start(f32[9,4,8,128]{3,2,1,0:T(8,128)S(1)} %collective-permute-done.axial_lo_ref) | copy-start | bytes 442372
  13.9 4.1 %copy-start.7 = (s32[32,8]{0,1:T(8,128)S(1)}, s32[32,8]{0,1:T(8,128)}, u32[]{:S(2)}) copy-start(s32[32,8]{0,1:T(8,128)} %param.8) | copy-start | bytes 3076
  13.9 4.3 %copy-start.1 = (s32[512]{0:T(512)S(1)}, s32[512]{0:T(512)}, u32[]{:S(2)}) copy-start(s32[512]{0:T(512)} %param.9) | copy-start | bytes 6148
  14.1 12.5 %collective-permute-start.2 = (f32[9,40,4,128]{3,2,1,0:T(4,128)S(1)}, f32[9,40,4,128]{3,2,1,0:T(4,128)S(1)}, u32[]{:S(2)}, u32[]{:S(2)}) collective-permute-start(f32[9,40,4,128]{3,2,1,0:T(4,128)S(1)} %pad_maximum_fusion.1), channel_id=1, source_target_pairs={{1,0},{2,1},{3,2},{4,3},{5,4},{6,5},{7,6},{8,7},{9,8},{10,9},{11,1... | collective-permute-start | bytes 2211848 | tf_op jit(solution)/shard_map/ppermute | solution.py:117
  17.9 13.7 %collective-permute-start.3 = (f32[9,40,4,128]{3,2,1,0:T(4,128)S(1)}, f32[9,40,4,128]{3,2,1,0:T(4,128)S(1)}, u32[]{:S(2)}, u32[]{:S(2)}) collective-permute-start(f32[9,40,4,128]{3,2,1,0:T(4,128)S(1)} %pad_maximum_fusion.2), channel_id=1, source_target_pairs={{0,1},{1,2},{2,3},{3,4},{4,5},{5,6},{6,7},{7,8},{8,9},{9,10},{10,1... | collective-permute-start | bytes 2211848 | tf_op jit(solution)/shard_map/ppermute | solution.py:114

commit v2 on v1

--- a/solution.py
+++ b/solution.py
@@ -8,6 +8,7 @@
 from jax.sharding import PartitionSpec as P
 
 ITERS = 4
+UNROLL = 4
 
 
 mach_number = 0.5
@@ -18,7 +19,7 @@
     axial_local, azim_local, radial_count, width, axial_total,
     axis_ref, state_ref, adjoint_ref, liner_ref, axial_lo_ref, axial_hi_ref, azim_ref,
     out_ref, grad_ref,
-    field_a, field_b, adj_a, adj_b, liner_pad, walls,
+    field_a, field_b, adj_a, adj_b, liner_pad, walls, adj_walls,
 ):
     rows = axial_local + 2 * width
     cols = azim_local + 2 * width
@@ -48,40 +49,50 @@
     def azim_diff(x):
         return (pltpu.roll(x, cols - 1, 0) - pltpu.roll(x, 1, 0)) * 0.5
 
-    def advance(src, dst, step, orient):
+    def row(src, dst, r, orient, keep):
+        centre = src[:, r]
+        along = (src[:, r + 1] - src[:, r - 1]) * 0.5
+        press, axial, azim, radial = centre[0], centre[1], centre[2], centre[3]
+        rate_press = (
+            orient * (-mach_number * along[0] - along[1] - azim_diff(azim) - radial_diff(radial))
+            - liner_pad[r] * press
+        )
+        rate_axial = orient * (-mach_number * along[1] - along[0])
+        rate_azim = orient * (-mach_number * along[2] - azim_diff(press))
+        rate_radial = orient * (-mach_number * along[3] - radial_diff(press))
+        dst[0, r] = (press + time_step * rate_press) * keep
+        dst[1, r] = (axial + time_step * rate_axial) * keep
+        dst[2, r] = (azim + time_step * rate_azim) * keep
+        dst[3, r] = (radial + time_step * rate_radial) * keep
+
+    def advance(chains, step):
         def body(r, carry):
-            centre = src[:, r]
-            along = (src[:, r + 1] - src[:, r - 1]) * 0.5
-            press, axial, azim, radial = centre[0], centre[1], centre[2], centre[3]
-            rate_press = (
-                orient * (-mach_number * along[0] - along[1] - azim_diff(azim) - radial_diff(radial))
-                - liner_pad[r] * press
-            )
-            rate_axial = orient * (-mach_number * along[1] - along[0])
-            rate_azim = orient * (-mach_number * along[2] - azim_diff(press))
-            rate_radial = orient * (-mach_number * along[3] - radial_diff(press))
             g = first_row + r
             keep = jnp.where((g >= 0) & (g < axial_total), 1.0, 0.0)
-            dst[0, r] = (press + time_step * rate_press) * keep
-            dst[1, r] = (axial + time_step * rate_axial) * keep
-            dst[2, r] = (azim + time_step * rate_azim) * keep
-            dst[3, r] = (radial + time_step * rate_radial) * keep
+            for src, dst, orient in chains:
+                row(src, dst, r, orient, keep)
             return carry
 
-        lax.fori_loop(step, rows - step, body, 0)
+        lax.fori_loop(step, rows - step, body, 0, unroll=UNROLL)
 
     walls[0] = state_ref[0]
-    bufs = (field_a, field_b)
-    for step in range(1, ITERS):
-        advance(bufs[(step - 1) % 2], bufs[step % 2], step, 1.0)
-        walls[step] = bufs[step % 2][0, own, own_cols]
+    adj_walls[0] = adjoint_ref[0]
+    fwd = (field_a, field_b)
+    adj = (adj_a, adj_b)
+    for step in range(1, ITERS + 1):
+        chains = [(adj[(step - 1) % 2], adj[step % 2], -1.0)]
+        if step < ITERS:
+            chains.append((fwd[(step - 1) % 2], fwd[step % 2], 1.0))
+        advance(chains, step)
+        if step < ITERS:
+            walls[step] = fwd[step % 2][0, own, own_cols]
+            adj_walls[step] = adj[step % 2][0, own, own_cols]
 
-    grad_ref[...] = jnp.zeros(grad_ref.shape, jnp.float32)
-    bufs = (adj_a, adj_b)
+    grad = jnp.zeros(grad_ref.shape, jnp.float32)
     for step in range(1, ITERS + 1):
-        grad_ref[...] = grad_ref[...] - time_step * bufs[(step - 1) % 2][0, own, own_cols] * walls[ITERS - step]
-        advance(bufs[(step - 1) % 2], bufs[step % 2], step, -1.0)
-    out_ref[...] = bufs[ITERS % 2][:, own, own_cols]
+        grad = grad - time_step * adj_walls[step - 1] * walls[ITERS - step]
+    grad_ref[...] = grad
+    out_ref[...] = adj[ITERS % 2][:, own, own_cols]
 
 
 def shards(state, final_adjoint, resistance, wall_patch, patch_slot_index):
@@ -136,6 +147,7 @@
         + [
             pltpu.VMEM((rows, cols, radial_count), jnp.float32),
             pltpu.VMEM((ITERS, axial_local, azim_local, radial_count), jnp.float32),
+            pltpu.VMEM((ITERS, axial_local, azim_local, radial_count), jnp.float32),
         ],
     )(axis_index, state, final_adjoint, liner, axial_lo, axial_hi, azim_halo)
     cell_grad = grad[:, :, radial_count - 1]

time: 76.1 us -> 60.3 us (0.79)
  Pallas kernels: 23.9 us -> 8.07 us
    pallas_call x1, Pallas kernels: 23.9 us -> 8.07 us  [shards(): pl.pallas_call(kernel, out_shape=(jax.ShapeDtypeStruct(state.shape, jnp.f...]
  transfers between devices with their start and end apart: 4 -> 4, of which waited for: 4 -> 4; matrix products, arithmetic and copies ran while one was open for 3% -> 4% of each run, Pallas kernels for 0% -> 0%
where the time goes in v2:
time: 60.3 us; the launch traced here: 60 us
  blocking collectives  16.3 us (27%)
  waiting for transfers between devices  14.3 us (24%)
  starting transfers between devices  9.8 us (16%)
  Pallas kernels  8.07 us (13%)
  local copies, waits for them, and re-layouts  5.43 us (9%)
  matrix products  2.68 us (4%)
  other arithmetic  2.51 us (4%)
  between operations  0.89 us (1%)
    all_to_all x1, blocking collectives, shards(): patch_gradient = lax.all_to_all(send, ('ax', 'az'), 0, 0, tiled=True).sum(0)  16.3 us
    pallas_call x1, Pallas kernels, shards(): pl.pallas_call(kernel, out_shape=(jax.ShapeDtypeStruct(state.shape, jnp.f...  8.07 us
    ppermute x1, waiting for transfers between devices, shards(): lax.ppermute(azim_pack(0, width), 'az', [((i + 1) % az_count, i) for i in...  6.52 us
    ppermute x1, waiting for transfers between devices, shards(): lax.ppermute(azim_pack(azim_local - width, azim_local), 'az', [(i, (i + 1...  4.97 us
    ppermute x1, starting transfers between devices, shards(): lax.ppermute(pack(1, axial_local - width, axial_local), 'ax', [(i, i + 1)...  4.89 us
    ppermute x1, starting transfers between devices, shards(): lax.ppermute(azim_pack(0, width), 'az', [((i + 1) % az_count, i) for i in...  3.57 us
    gather x1, local copies, waits for them, and re-layouts, shards(): cell_slot = patch_slot_index[wall_patch].reshape(-1)  1.95 us
    dot_general x1, matrix products, shards(): damping = jnp.dot(patch_onehot, resistance, precision=lax.Precision.HIGHEST)  1.9 us
  transfers between devices with their start and end apart: 4, of which 4 were waited for; matrix products, arithmetic and copies ran while one was open for 4% of the time, Pallas kernels for 0%

profile of v2, /device:TPU:0, one launch (start us, length us, event | category | flops | bytes accessed | tf_op | source)
XLA Modules:
  0.0 60.0 jit_solution(10271252346514484736)
XLA Ops:
  0.6 0.0 copy-start
  0.6 0.0 copy-start.2
  0.7 0.0 copy-start.3
  0.7 0.8 %copy.10 = s32[32,8]{1,0:T(8,128)S(1)} copy(s32[32,8]{0,1:T(8,128)} %param.8) | data formatting | bytes 2048 | tf_op args[3]
  1.5 0.0 copy-done
  1.5 1.9 %fusion.4 = f32[1,32,8]{2,0,1:T(1,128)S(1)} fusion(f32[512,1,1]{0,1,2:T(1,128)S(1)} %bitcast.17, s32[32,8]{1,0:T(8,128)S(1)} %copy.10), kind=kOutput, calls=%fused_computation.9 | convolution fusion | flops 1703936 | bytes 4096 | tf_op jit(solution)/shard_map/dot_general | solution.py:106
  3.4 0.1 broadcast_multiply_fusion.liner_ref
  3.5 0.0 copy-start.4
  3.6 1.0 %fusion.8 = (f32[4,4,8,128]{3,2,1,0:T(8,128)S(1)}, f32[4,4,8,128]{3,2,1,0:T(8,128)S(1)}, f32[4,4,8,128]{3,2,1,0:T(8,128)S(1)}, f32[4,4,8,128]{3,2,1,0:T(8,128)S(1)}) fusion(f32[4,32,8,128]{3,2,1,0:T(8,128)} %state_ref.1, f32[4,32,8,128]{3,2,1,0:T(8,128)} %adjoint_ref.1), kind=kLoop, calls=%fused_computation.25 | loop fusion | bytes 524288 | tf_op jit(solution)/shard_map/slice | solution.py:110
  4.6 1.3 %collective-permute-start.1 = (f32[9,4,8,128]{3,2,1,0:T(8,128)S(1)}, f32[9,4,8,128]{3,2,1,0:T(8,128)S(1)}, u32[]{:S(2)}, u32[]{:S(2)}) collective-permute-start(f32[9,4,8,128]{3,2,1,0:T(8,128)S(1)} %pad_maximum_fusion.4), channel_id=1, source_target_pairs={{16,0},{17,1},{18,2},{19,3},{20,4},{21,5},{22,6},{23,7},{24,8},{25... | collective-permute-start | bytes 442376 | tf_op jit(solution)/shard_map/ppermute | solution.py:118
  5.9 4.9 %collective-permute-start = (f32[9,4,8,128]{3,2,1,0:T(8,128)S(1)}, f32[9,4,8,128]{3,2,1,0:T(8,128)S(1)}, u32[]{:S(2)}, u32[]{:S(2)}) collective-permute-start(f32[9,4,8,128]{3,2,1,0:T(8,128)S(1)} %pad_maximum_fusion.3), channel_id=1, source_target_pairs={{0,16},{1,17},{2,18},{3,19},{4,20},{5,21},{6,22},{7,23},{8,24},{9,... | collective-permute-start | bytes 442376 | tf_op jit(solution)/shard_map/ppermute | solution.py:116
  10.8 0.0 copy-done.2
  10.8 0.0 copy-done.3
  10.8 0.2 fusion.6
  11.0 0.0 copy-done.4
  11.1 1.6 %collective-permute-done.1.axial_hi_ref = f32[9,4,8,128]{3,2,1,0:T(8,128)S(1)} collective-permute-done((f32[9,4,8,128]{3,2,1,0:T(8,128)S(1)}, f32[9,4,8,128]{3,2,1,0:T(8,128)S(1)}, u32[]{:S(2)}, u32[]{:S(2)}) %collective-permute-start.1) | collective-permute-done | bytes 147488 | tf_op jit(solution)/shard_map/ppermute | solution.py:118
  12.7 0.0 copy-start.5
  12.7 1.2 %collective-permute-done.axial_lo_ref = f32[9,4,8,128]{3,2,1,0:T(8,128)S(1)} collective-permute-done((f32[9,4,8,128]{3,2,1,0:T(8,128)S(1)}, f32[9,4,8,128]{3,2,1,0:T(8,128)S(1)}, u32[]{:S(2)}, u32[]{:S(2)}) %collective-permute-start) | collective-permute-done | bytes 147488 | tf_op jit(solution)/shard_map/ppermute | solution.py:116
  13.9 0.0 copy-start.6
  13.9 0.0 copy-start.7
  13.9 0.0 copy-start.1
  13.9 0.2 pad_maximum_fusion.1
  14.1 3.6 %collective-permute-start.2 = (f32[9,40,4,128]{3,2,1,0:T(4,128)S(1)}, f32[9,40,4,128]{3,2,1,0:T(4,128)S(1)}, u32[]{:S(2)}, u32[]{:S(2)}) collective-permute-start(f32[9,40,4,128]{3,2,1,0:T(4,128)S(1)} %pad_maximum_fusion.1), channel_id=1, source_target_pairs={{1,0},{2,1},{3,2},{4,3},{5,4},{6,5},{7,6},{8,7},{9,8},{10,9},{11,1... | collective-permute-start | bytes 2211848 | tf_op jit(solution)/shard_map/ppermute | solution.py:128
  17.7 0.2 pad_maximum_fusion.2
  17.9 0.0 copy-done.5
  17.9 0.0 copy-done.6
  17.9 0.1 collective-permute-start.3
  18.0 0.0 copy-done.7
  18.0 0.1 copy.11
  18.1 0.1 reshape.46
  18.2 0.0 copy-done.1
  18.2 1.9 %gather_fusion = s32[256]{0:T(256)S(1)} fusion(s32[512]{0:T(512)S(1)} %copy-done.1, s32[1024]{0:T(1024)S(1)} %pad_clamp_fusion), kind=kCustom, calls=%fused_computation | custom fusion | bytes 3072 | tf_op jit(solution)/shard_map/gather | solution.py:156
  20.2 6.5 %collective-permute-done.2 = f32[9,40,4,128]{3,2,1,0:T(4,128)S(1)} collective-permute-done((f32[9,40,4,128]{3,2,1,0:T(4,128)S(1)}, f32[9,40,4,128]{3,2,1,0:T(4,128)S(1)}, u32[]{:S(2)}, u32[]{:S(2)}) %collective-permute-start.2) | collective-permute-done | bytes 737312 | tf_op jit(solution)/shard_map/ppermute | solution.py:128
  26.7 5.0 %collective-permute-done.3 = f32[9,40,4,128]{3,2,1,0:T(4,128)S(1)} collective-permute-done((f32[9,40,4,128]{3,2,1,0:T(4,128)S(1)}, f32[9,40,4,128]{3,2,1,0:T(4,128)S(1)}, u32[]{:S(2)}, u32[]{:S(2)}) %collective-permute-start.3) | collective-permute-done | bytes 737312 | tf_op jit(solution)/shard_map/ppermute | solution.py:125
  31.7 1.4 %pad_maximum_fusion.azim_ref = f32[9,40,8,128]{3,2,1,0:T(8,128)} fusion(f32[9,40,4,128]{3,2,1,0:T(4,128)S(1)} %collective-permute-done.3, f32[9,40,4,128]{3,2,1,0:T(4,128)S(1)} %collective-permute-done.2), kind=kLoop, calls=%fused_computation.1 | loop fusion | flops 368640 | bytes 2949120 | tf_op jit(solution)/shard_map/concatenate | solution.py:129
  33.1 8.1 %shard_map.68 = (f32[4,32,8,128]{3,2,1,0:T(8,128)}, f32[32,8,128]{2,1,0:T(8,128)}) custom-call(s32[1]{0:T(128)} %bitcast.axis_ref, f32[4,32,8,128]{3,2,1,0:T(8,128)} %state_ref.1, f32[4,32,8,128]{3,2,1,0:T(8,128)} %adjoint_ref.1, f32[32,8,128]{2,1,0:T(8,128)} %copy-done.4, f32[9,4,8,128]{3,2,1,0:T(8,128)} %copy-done.6, f32[9,4,8,128]{3,2,1,0:T(8,128)} %copy-done.5, ...), custom_call_target="tpu_custom_call" | custom-call | tf_op jit(solution)/shard_map/pallas_call | solution.py:138
  41.2 1.1 %slice_reduce_fusion = f32[32,8]{1,0:T(8,128)S(1)} fusion(f32[32,8,128]{2,1,0:T(8,128)} %get-tuple-element.5), kind=kLoop, calls=%fused_computation.13 | loop fusion | bytes 2048 | tf_op jit(solution)/shard_map/slice | solution.py:153
  42.2 0.1 reshape.57
  42.3 0.8 %fusion = f32[1,16,64]{2,0,1:T(1,128)S(1)} fusion(f32[256,1,1]{0,1,2:T(1,128)S(1)} %reshape.57, s32[256]{0:T(256)S(1)} %gather_fusion, s32[16,64]{1,0:T(8,128)S(1)} %multiply_add_fusion), kind=kOutput, calls=%fused_computation.2 | convolution fusion | flops 3407872 | bytes 10240 | tf_op jit(solution)/shard_map/dot_general | solution.py:158
  43.1 16.3 %all_to_all.9 = f32[32,1,64]{2,1,0:T(1,128)S(1)} all-to-all(f32[32,1,64]{2,1,0:T(1,128)S(1)} %bitcast.18), channel_id=1, replica_groups=mesh['ax'=2,'az'=16] {'ax','az'}, dimensions={0} | all-to-all | bytes 16384 | tf_op jit(solution)/shard_map/all_to_all | solution.py:161
  59.4 0.6 reduce_sum.9
  (11 shorter events, 0.1 us)
Async XLA Ops:
  0.6 0.9 %copy-start = (f32[512]{0:T(512)S(1)}, f32[512]{0:T(512)}, u32[]{:S(2)}) copy-start(f32[512]{0:T(512)} %param.7) | copy-start | bytes 6148
  0.6 10.2 %copy-start.2 = (f32[4,32,8,128]{3,2,1,0:T(8,128)S(1)}, f32[4,32,8,128]{3,2,1,0:T(8,128)}, u32[]{:S(2)}) copy-start(f32[4,32,8,128]{3,2,1,0:T(8,128)} %state_ref.1) | copy-start | bytes 1572868
  0.7 10.2 %copy-start.3 = (f32[4,32,8,128]{3,2,1,0:T(8,128)S(1)}, f32[4,32,8,128]{3,2,1,0:T(8,128)}, u32[]{:S(2)}) copy-start(f32[4,32,8,128]{3,2,1,0:T(8,128)} %adjoint_ref.1) | copy-start | bytes 1572868
  3.5 7.5 %copy-start.4 = (f32[32,8,128]{2,1,0:T(8,128)}, f32[32,8,128]{2,1,0:T(8,128)S(1)}, u32[]{:S(2)}) copy-start(f32[32,8,128]{2,1,0:T(8,128)S(1)} %broadcast_multiply_fusion.liner_ref) | copy-start | bytes 393220
  4.6 8.1 %collective-permute-start.1 = (f32[9,4,8,128]{3,2,1,0:T(8,128)S(1)}, f32[9,4,8,128]{3,2,1,0:T(8,128)S(1)}, u32[]{:S(2)}, u32[]{:S(2)}) collective-permute-start(f32[9,4,8,128]{3,2,1,0:T(8,128)S(1)} %pad_maximum_fusion.4), channel_id=1, source_target_pairs={{16,0},{17,1},{18,2},{19,3},{20,4},{21,5},{22,6},{23,7},{24,8},{25... | collective-permute-start | bytes 442376 | tf_op jit(solution)/shard_map/ppermute | solution.py:118
  5.9 8.0 %collective-permute-start = (f32[9,4,8,128]{3,2,1,0:T(8,128)S(1)}, f32[9,4,8,128]{3,2,1,0:T(8,128)S(1)}, u32[]{:S(2)}, u32[]{:S(2)}) collective-permute-start(f32[9,4,8,128]{3,2,1,0:T(8,128)S(1)} %pad_maximum_fusion.3), channel_id=1, source_target_pairs={{0,16},{1,17},{2,18},{3,19},{4,20},{5,21},{6,22},{7,23},{8,24},{9,... | collective-permute-start | bytes 442376 | tf_op jit(solution)/shard_map/ppermute | solution.py:116
  12.7 5.2 %copy-start.5 = (f32[9,4,8,128]{3,2,1,0:T(8,128)}, f32[9,4,8,128]{3,2,1,0:T(8,128)S(1)}, u32[]{:S(2)}) copy-start(f32[9,4,8,128]{3,2,1,0:T(8,128)S(1)} %collective-permute-done.1.axial_hi_ref) | copy-start | bytes 442372
  13.9 4.0 %copy-start.6 = (f32[9,4,8,128]{3,2,1,0:T(8,128)}, f32[9,4,8,128]{3,2,1,0:T(8,128)S(1)}, u32[]{:S(2)}) copy-start(f32[9,4,8,128]{3,2,1,0:T(8,128)S(1)} %collective-permute-done.axial_lo_ref) | copy-start | bytes 442372
  13.9 4.1 %copy-start.7 = (s32[32,8]{0,1:T(8,128)S(1)}, s32[32,8]{0,1:T(8,128)}, u32[]{:S(2)}) copy-start(s32[32,8]{0,1:T(8,128)} %param.8) | copy-start | bytes 3076
  13.9 4.3 %copy-start.1 = (s32[512]{0:T(512)S(1)}, s32[512]{0:T(512)}, u32[]{:S(2)}) copy-start(s32[512]{0:T(512)} %param.9) | copy-start | bytes 6148
  14.1 12.5 %collective-permute-start.2 = (f32[9,40,4,128]{3,2,1,0:T(4,128)S(1)}, f32[9,40,4,128]{3,2,1,0:T(4,128)S(1)}, u32[]{:S(2)}, u32[]{:S(2)}) collective-permute-start(f32[9,40,4,128]{3,2,1,0:T(4,128)S(1)} %pad_maximum_fusion.1), channel_id=1, source_target_pairs={{1,0},{2,1},{3,2},{4,3},{5,4},{6,5},{7,6},{8,7},{9,8},{10,9},{11,1... | collective-permute-start | bytes 2211848 | tf_op jit(solution)/shard_map/ppermute | solution.py:128
  17.9 13.7 %collective-permute-start.3 = (f32[9,40,4,128]{3,2,1,0:T(4,128)S(1)}, f32[9,40,4,128]{3,2,1,0:T(4,128)S(1)}, u32[]{:S(2)}, u32[]{:S(2)}) collective-permute-start(f32[9,40,4,128]{3,2,1,0:T(4,128)S(1)} %pad_maximum_fusion.2), channel_id=1, source_target_pairs={{0,1},{1,2},{2,3},{3,4},{4,5},{5,6},{6,7},{7,8},{8,9},{9,10},{10,1... | collective-permute-start | bytes 2211848 | tf_op jit(solution)/shard_map/ppermute | solution.py:125

commit v3 on v2

--- a/solution.py
+++ b/solution.py
@@ -17,24 +17,30 @@
 
 def steps_kernel(
     axial_local, azim_local, radial_count, width, axial_total,
-    axis_ref, state_ref, adjoint_ref, liner_ref, axial_lo_ref, axial_hi_ref, azim_ref,
+    axis_ref, state_ref, adjoint_ref, liner_ref,
+    state_lo_ref, state_hi_ref, adj_lo_ref, adj_hi_ref,
+    state_next_ref, state_prev_ref, adj_next_ref, adj_prev_ref,
     out_ref, grad_ref,
-    field_a, field_b, adj_a, adj_b, liner_pad, walls, adj_walls,
+    field_a, field_b, adj_a, adj_b, walls, adj_walls,
 ):
     rows = axial_local + 2 * width
     cols = azim_local + 2 * width
     own = slice(width, width + axial_local)
     own_cols = slice(0, azim_local)
+    liner_pad = liner_ref
+    narrow = width - 1
 
-    for buf, lo in ((field_a, 0), (adj_a, 4)):
-        buf[:, own, own_cols] = state_ref[...] if lo == 0 else adjoint_ref[...]
-        buf[:, 0:width, own_cols] = axial_lo_ref[lo : lo + 4]
-        buf[:, width + axial_local : rows, own_cols] = axial_hi_ref[lo : lo + 4]
-        buf[:, :, azim_local:cols] = azim_ref[lo : lo + 4]
-    liner_pad[own, own_cols] = liner_ref[...]
-    liner_pad[0:width, own_cols] = axial_lo_ref[8]
-    liner_pad[width + axial_local : rows, own_cols] = axial_hi_ref[8]
-    liner_pad[:, azim_local:cols] = azim_ref[8]
+    field_a[...] = jnp.zeros(field_a.shape, jnp.float32)
+    field_a[:, own, own_cols] = state_ref[...]
+    field_a[:, 1:width, own_cols] = state_lo_ref[...]
+    field_a[:, width + axial_local : rows - 1, own_cols] = state_hi_ref[...]
+    field_a[:, 1 : rows - 1, azim_local : azim_local + narrow] = state_next_ref[...]
+    field_a[:, 1 : rows - 1, cols - narrow : cols] = state_prev_ref[...]
+    adj_a[:, own, own_cols] = adjoint_ref[...]
+    adj_a[:, 0:width, own_cols] = adj_lo_ref[...]
+    adj_a[:, width + axial_local : rows, own_cols] = adj_hi_ref[...]
+    adj_a[:, :, azim_local : azim_local + width] = adj_next_ref[...]
+    adj_a[:, :, azim_local + width : cols] = adj_prev_ref[...]
 
     first_row = axis_ref[0] * axial_local - width
     lane = lax.broadcasted_iota(jnp.int32, (cols, radial_count), 1)
@@ -100,33 +106,43 @@
     axial_local = state.shape[1]
     azim_local = state.shape[2]
     radial_count = state.shape[3]
-    wall = (jnp.arange(radial_count) == radial_count - 1).astype(jnp.float32)
+    narrow = width - 1
+    ax_count = lax.axis_size("ax")
+    az_count = lax.axis_size("az")
+    up_ax = [(i, i + 1) for i in range(ax_count - 1)]
+    down_ax = [(i + 1, i) for i in range(ax_count - 1)]
+    up_az = [(i, (i + 1) % az_count) for i in range(az_count)]
+    down_az = [((i + 1) % az_count, i) for i in range(az_count)]
+
+    def tail(x, dim, n):
+        return lax.slice_in_dim(x, x.shape[dim] - n, x.shape[dim], axis=dim)
+
+    def head(x, dim, n):
+        return lax.slice_in_dim(x, 0, n, axis=dim)
+
+    state_lo = lax.ppermute(tail(state, 1, narrow), "ax", up_ax)
+    adj_lo = lax.ppermute(tail(final_adjoint, 1, width), "ax", up_ax)
+    state_hi = lax.ppermute(head(state, 1, narrow), "ax", down_ax)
+    adj_hi = lax.ppermute(head(final_adjoint, 1, width), "ax", down_ax)
+
     patch_count = resistance.shape[0]
     patch_onehot = (wall_patch[:, :, None] == jnp.arange(patch_count, dtype=jnp.int32)).astype(jnp.float32)
     damping = jnp.dot(patch_onehot, resistance, precision=lax.Precision.HIGHEST)
-    liner = damping[:, :, None] * wall[None, None, :]
+    damp_lo = lax.ppermute(tail(damping, 0, width), "ax", up_ax)
+    damp_hi = lax.ppermute(head(damping, 0, width), "ax", down_ax)
 
-    def pack(sl_axis, start, stop):
-        parts = [lax.slice_in_dim(x, start, stop, axis=sl_axis) for x in (state, final_adjoint)]
-        parts.append(lax.slice_in_dim(liner, start, stop, axis=sl_axis - 1)[None])
-        return jnp.concatenate(parts, axis=0)
-
-    ax_count = lax.axis_size("ax")
-    az_count = lax.axis_size("az")
-    axial_lo, axial_hi = lax.ppermute(
-        pack(1, axial_local - width, axial_local), "ax", [(i, i + 1) for i in range(ax_count - 1)]
-    ), lax.ppermute(pack(1, 0, width), "ax", [(i + 1, i) for i in range(ax_count - 1)])
-
-    def azim_pack(start, stop):
-        return jnp.concatenate(
-            [axial_lo[:, :, start:stop], pack(2, start, stop), axial_hi[:, :, start:stop]], axis=1
-        )
-
-    azim_prev = lax.ppermute(
-        azim_pack(azim_local - width, azim_local), "az", [(i, (i + 1) % az_count) for i in range(az_count)]
-    )
-    azim_next = lax.ppermute(azim_pack(0, width), "az", [((i + 1) % az_count, i) for i in range(az_count)])
-    azim_halo = jnp.concatenate([azim_next, azim_prev], axis=2)
+    state_rows = jnp.concatenate([state_lo, state, state_hi], axis=1)
+    adj_rows = jnp.concatenate([adj_lo, final_adjoint, adj_hi], axis=1)
+    damp_rows = jnp.concatenate([damp_lo, damping, damp_hi], axis=0)
+    state_prev = lax.ppermute(tail(state_rows, 2, narrow), "az", up_az)
+    adj_prev = lax.ppermute(tail(adj_rows, 2, width), "az", up_az)
+    state_next = lax.ppermute(head(state_rows, 2, narrow), "az", down_az)
+    adj_next = lax.ppermute(head(adj_rows, 2, width), "az", down_az)
+    damp_prev = lax.ppermute(tail(damp_rows, 1, width), "az", up_az)
+    damp_next = lax.ppermute(head(damp_rows, 1, width), "az", down_az)
+    damp_pad = jnp.concatenate([damp_rows, damp_next, damp_prev], axis=1)
+    wall = (jnp.arange(radial_count) == radial_count - 1).astype(jnp.float32)
+    liner_pad = damp_pad[:, :, None] * wall[None, None, :]
 
     rows = axial_local + 2 * width
     cols = azim_local + 2 * width
@@ -141,15 +157,18 @@
             jax.ShapeDtypeStruct(state.shape, jnp.float32),
             jax.ShapeDtypeStruct((axial_local, azim_local, radial_count), jnp.float32),
         ),
-        in_specs=[pl.BlockSpec(memory_space=pltpu.SMEM)] + [vmem] * 6,
+        in_specs=[pl.BlockSpec(memory_space=pltpu.SMEM)] + [vmem] * 11,
         out_specs=(vmem, vmem),
         scratch_shapes=[pltpu.VMEM((4, rows, cols, radial_count), jnp.float32)] * 4
         + [
-            pltpu.VMEM((rows, cols, radial_count), jnp.float32),
             pltpu.VMEM((ITERS, axial_local, azim_local, radial_count), jnp.float32),
             pltpu.VMEM((ITERS, axial_local, azim_local, radial_count), jnp.float32),
         ],
-    )(axis_index, state, final_adjoint, liner, axial_lo, axial_hi, azim_halo)
+    )(
+        axis_index, state, final_adjoint, liner_pad,
+        state_lo, state_hi, adj_lo, adj_hi,
+        state_next, state_prev, adj_next, adj_prev,
+    )
     cell_grad = grad[:, :, radial_count - 1]
 
     slot_total = 2 * resistance.shape[0]

time: 60.3 us -> 71.1 us (1.18)
  starting transfers between devices: 9.8 us -> 26.9 us
  waiting for transfers between devices: 14.3 us -> 9.52 us
  blocking collectives: 16.3 us -> 11.6 us
  local copies, waits for them, and re-layouts: 5.43 us -> 9.34 us
  other arithmetic: 2.51 us -> 1.62 us
    ppermute x4 -> x12, starting transfers between devices: 9.8 us -> 26.9 us  [the longest x1 4.88 us: shards(): damp_lo = lax.ppermute(tail(damping, 0, width), 'ax', up_ax)]
    ppermute x4 -> x12, waiting for transfers between devices: 14.3 us -> 9.52 us  [the longest x1 4.6 us: shards(): adj_prev = lax.ppermute(tail(adj_rows, 2, width), 'az', up_az)]
    all_to_all x1, blocking collectives: 16.3 us -> 11.6 us  [shards(): patch_gradient = lax.all_to_all(send, ('ax', 'az'), 0, 0, tiled=True).sum(0)]
    unnamed x17 -> x31, local copies, waits for them, and re-layouts: 0.89 us -> 4.73 us
    concatenate x5 -> x2, other arithmetic: 1.81 us -> 0.15 us  [the longest x1 0.08 us: shards(): damp_pad = jnp.concatenate([damp_rows, damp_next, damp_prev], axis=1)]
    mul x1, other arithmetic: 0.11 us -> 0.89 us  [shards(): liner_pad = damp_pad[:, :, None] * wall[None, None, :]]
  transfers between devices with their start and end apart: 4 -> 12, of which waited for: 4 -> 4; matrix products, arithmetic and copies ran while one was open for 4% -> 6% of each run, Pallas kernels for 0% -> 0%
where the time goes in v3:
time: 71.1 us; the launch traced here: 70.7 us
  starting transfers between devices  26.9 us (38%)
  blocking collectives  11.6 us (16%)
  waiting for transfers between devices  9.52 us (13%)
  local copies, waits for them, and re-layouts  9.34 us (13%)
  Pallas kernels  8.13 us (11%)
  matrix products  2.68 us (4%)
  other arithmetic  1.62 us (2%)
  between operations  0.9 us (1%)
    all_to_all x1, blocking collectives, shards(): patch_gradient = lax.all_to_all(send, ('ax', 'az'), 0, 0, tiled=True).sum(0)  11.6 us
    pallas_call x1, Pallas kernels, shards(): pl.pallas_call(kernel, out_shape=(jax.ShapeDtypeStruct(state.shape, jnp.f...  8.13 us
    ppermute x1, starting transfers between devices, shards(): damp_lo = lax.ppermute(tail(damping, 0, width), 'ax', up_ax)  4.88 us
    unnamed x31, local copies, waits for them, and re-layouts  4.73 us
    ppermute x1, waiting for transfers between devices, shards(): adj_prev = lax.ppermute(tail(adj_rows, 2, width), 'az', up_az)  4.6 us
    ppermute x1, starting transfers between devices, shards(): state_lo = lax.ppermute(tail(state, 1, narrow), 'ax', up_ax)  4.55 us
    ppermute x1, starting transfers between devices, shards(): adj_lo = lax.ppermute(tail(final_adjoint, 1, width), 'ax', up_ax)  4.55 us
    ppermute x1, starting transfers between devices, shards(): adj_next = lax.ppermute(head(adj_rows, 2, width), 'az', down_az)  3.89 us
  transfers between devices with their start and end apart: 12, of which 4 were waited for; matrix products, arithmetic and copies ran while one was open for 6% of the time, Pallas kernels for 0%

profile of v3, /device:TPU:0, one launch (start us, length us, event | category | flops | bytes accessed | tf_op | source)
XLA Modules:
  0.0 70.7 jit_solution(1091563240577991163)
XLA Ops:
  0.6 0.0 copy-start
  0.6 0.0 copy-start.3
  0.7 0.8 %copy.10 = s32[32,8]{1,0:T(8,128)S(1)} copy(s32[32,8]{0,1:T(8,128)} %param.8) | data formatting | bytes 2048 | tf_op args[3]
  1.5 0.0 copy-done
  1.5 1.9 %fusion.4 = f32[1,32,8]{2,0,1:T(1,128)S(1)} fusion(f32[512,1,1]{0,1,2:T(1,128)S(1)} %bitcast.8, s32[32,8]{1,0:T(8,128)S(1)} %copy.10), kind=kOutput, calls=%fused_computation.6 | convolution fusion | flops 1703936 | bytes 4096 | tf_op jit(solution)/shard_map/dot_general | solution.py:130
  3.4 0.1 copy.13
  3.4 0.1 fusion.11
  3.5 4.9 %collective-permute-start = (f32[4,8]{0,1:T(8,128)S(1)}, f32[4,8]{0,1:T(8,128)S(1)}, u32[]{:S(2)}, u32[]{:S(2)}) collective-permute-start(f32[4,8]{0,1:T(8,128)S(1)} %get-tuple-element.16), channel_id=1, source_target_pairs={{0,16},{1,17},{2,18},{3,19},{4,20},{5,21},{6,22},{7,23},{8,24},{9,... | collective-permute-start | bytes 392 | tf_op jit(solution)/shard_map/ppermute | solution.py:131
  8.4 1.3 %collective-permute-start.1 = (f32[4,8]{0,1:T(8,128)S(1)}, f32[4,8]{0,1:T(8,128)S(1)}, u32[]{:S(2)}, u32[]{:S(2)}) collective-permute-start(f32[4,8]{0,1:T(8,128)S(1)} %get-tuple-element.17), channel_id=1, source_target_pairs={{16,0},{17,1},{18,2},{19,3},{20,4},{21,5},{22,6},{23,7},{24,8},{25... | collective-permute-start | bytes 392 | tf_op jit(solution)/shard_map/ppermute | solution.py:132
  9.7 0.9 %fusion.8 = (f32[4,4,8,128]{3,2,1,0:T(8,128)S(1)}, f32[4,4,8,128]{3,2,1,0:T(8,128)S(1)}) fusion(f32[4,32,8,128]{3,2,1,0:T(8,128)} %adjoint_ref.1), kind=kLoop, calls=%fused_computation.24 | loop fusion | bytes 262144 | tf_op jit(solution)/shard_map/slice | solution.py:121
  10.6 4.5 %collective-permute-start.6 = (f32[4,4,8,128]{3,2,1,0:T(8,128)S(1)}, f32[4,4,8,128]{3,2,1,0:T(8,128)S(1)}, u32[]{:S(2)}, u32[]{:S(2)}) collective-permute-start(f32[4,4,8,128]{3,2,1,0:T(8,128)S(1)} %get-tuple-element.11), channel_id=1, source_target_pairs={{0,16},{1,17},{2,18},{3,19},{4,20},{5,21},{6,22},{7,23},{8,24},{9,... | collective-permute-start | bytes 196616 | tf_op jit(solution)/shard_map/ppermute | solution.py:124
  15.2 1.3 %collective-permute-start.7 = (f32[4,4,8,128]{3,2,1,0:T(8,128)S(1)}, f32[4,4,8,128]{3,2,1,0:T(8,128)S(1)}, u32[]{:S(2)}, u32[]{:S(2)}) collective-permute-start(f32[4,4,8,128]{3,2,1,0:T(8,128)S(1)} %get-tuple-element.10), channel_id=1, source_target_pairs={{16,0},{17,1},{18,2},{19,3},{20,4},{21,5},{22,6},{23,7},{24,8},{25... | collective-permute-start | bytes 196616 | tf_op jit(solution)/shard_map/ppermute | solution.py:126
  16.5 0.0 copy-done.3
  16.5 0.0 copy-start.12
  16.5 4.5 %collective-permute-start.4 = (f32[4,3,8,128]{3,2,1,0:T(8,128)S(1)}, f32[4,3,8,128]{3,2,1,0:T(8,128)S(1)}, u32[]{:S(2)}, u32[]{:S(2)}) collective-permute-start(f32[4,3,8,128]{3,2,1,0:T(8,128)S(1)} %get-tuple-element.13), channel_id=1, source_target_pairs={{0,16},{1,17},{2,18},{3,19},{4,20},{5,21},{6,22},{7,23},{8,24},{9,... | collective-permute-start | bytes 147464 | tf_op jit(solution)/shard_map/ppermute | solution.py:123
  21.1 0.0 copy-done.12
  21.1 0.1 copy.12
  21.2 0.1 reshape.46
  21.3 0.0 copy-start.1
  21.3 0.7 copy-done.1
  22.0 1.9 %gather_fusion = s32[256]{0:T(256)S(1)} fusion(s32[512]{0:T(512)S(1)} %copy-done.1, s32[1024]{0:T(1024)S(1)} %pad_clamp_fusion), kind=kCustom, calls=%fused_computation | custom fusion | bytes 3072 | tf_op jit(solution)/shard_map/gather | solution.py:175
  23.9 0.0 collective-permute-done
  23.9 1.3 %collective-permute-start.5 = (f32[4,3,8,128]{3,2,1,0:T(8,128)S(1)}, f32[4,3,8,128]{3,2,1,0:T(8,128)S(1)}, u32[]{:S(2)}, u32[]{:S(2)}) collective-permute-start(f32[4,3,8,128]{3,2,1,0:T(8,128)S(1)} %get-tuple-element.12), channel_id=1, source_target_pairs={{16,0},{17,1},{18,2},{19,3},{20,4},{21,5},{22,6},{23,7},{24,8},{25... | collective-permute-start | bytes 147464 | tf_op jit(solution)/shard_map/ppermute | solution.py:125
  25.2 0.0 collective-permute-done.1
  25.2 0.1 pad_maximum_fusion.1
  25.3 2.6 %collective-permute-start.2 = (f32[40,4]{0,1:T(4,128)S(1)}, f32[40,4]{0,1:T(4,128)S(1)}, u32[]{:S(2)}, u32[]{:S(2)}) collective-permute-start(f32[40,4]{0,1:T(4,128)S(1)} %get-tuple-element.14), channel_id=1, source_target_pairs={{1,0},{2,1},{3,2},{4,3},{5,4},{6,5},{7,6},{8,7},{9,8},{10,9},{11,1... | collective-permute-start | bytes 1928 | tf_op jit(solution)/shard_map/ppermute | solution.py:142
  27.9 0.0 collective-permute-done.4.state_lo_ref
  27.9 0.0 copy-start.10
  27.9 0.0 collective-permute-start.3
  27.9 0.6 copy-done.10
  28.5 1.4 %collective-permute-done.5.state_hi_ref = f32[4,3,8,128]{3,2,1,0:T(8,128)S(1)} collective-permute-done((f32[4,3,8,128]{3,2,1,0:T(8,128)S(1)}, f32[4,3,8,128]{3,2,1,0:T(8,128)S(1)}, u32[]{:S(2)}, u32[]{:S(2)}) %collective-permute-start.5) | collective-permute-done | bytes 49184 | tf_op jit(solution)/shard_map/ppermute | solution.py:125
  29.9 0.0 copy-start.11
  29.9 0.6 copy-done.11
  30.5 0.1 fusion.7
  30.6 2.5 %collective-permute-start.8 = (f32[4,38,3,128]{3,2,1,0:T(4,128)S(1)}, f32[4,38,3,128]{3,2,1,0:T(4,128)S(1)}, u32[]{:S(2)}, u32[]{:S(2)}) collective-permute-start(f32[4,38,3,128]{3,2,1,0:T(4,128)S(1)} %get-tuple-element.9), channel_id=1, source_target_pairs={{1,0},{2,1},{3,2},{4,3},{5,4},{6,5},{7,6},{8,7},{9,8},{10,9},{11,1... | collective-permute-start | bytes 700424 | tf_op jit(solution)/shard_map/ppermute | solution.py:139
  33.2 0.0 collective-permute-done.6.adj_lo_ref
  33.2 0.0 collective-permute-start.9
  33.2 0.6 copy-done.8
  33.8 0.0 copy-done.2
  33.8 0.0 collective-permute-done.7.adj_hi_ref
  33.8 0.0 copy-start.9
  33.9 0.6 copy-done.9
  34.5 0.1 fusion.6
  34.6 3.9 %collective-permute-start.10 = (f32[4,40,4,128]{3,2,1,0:T(4,128)S(1)}, f32[4,40,4,128]{3,2,1,0:T(4,128)S(1)}, u32[]{:S(2)}, u32[]{:S(2)}) collective-permute-start(f32[4,40,4,128]{3,2,1,0:T(4,128)S(1)} %get-tuple-element.7), channel_id=1, source_target_pairs={{1,0},{2,1},{3,2},{4,3},{5,4},{6,5},{7,6},{8,7},{9,8},{10,9},{11,1... | collective-permute-start | bytes 983048 | tf_op jit(solution)/shard_map/ppermute | solution.py:140
  38.5 0.0 collective-permute-done.2
  38.5 0.0 collective-permute-start.11
  38.5 0.0 collective-permute-done.3
  38.5 0.1 pad_maximum_fusion
  38.5 0.1 copy.11
  38.6 0.9 %broadcast_multiply_fusion.liner_ref = f32[40,16,128]{2,1,0:T(8,128)} fusion(f32[128]{0:T(128)S(1)} %compare_convert_fusion, f32[40,16]{1,0:T(8,128)S(1)} %copy.11), kind=kLoop, calls=%fused_computation.8 | loop fusion | flops 81920 | bytes 330752 | tf_op jit(solution)/shard_map/mul | solution.py:145
  39.5 0.0 collective-permute-done.8.state_next_ref
  39.5 2.8 %collective-permute-done.9.state_prev_ref = f32[4,38,3,128]{3,2,1,0:T(4,128)S(1)} collective-permute-done((f32[4,38,3,128]{3,2,1,0:T(4,128)S(1)}, f32[4,38,3,128]{3,2,1,0:T(4,128)S(1)}, u32[]{:S(2)}, u32[]{:S(2)}) %collective-permute-start.9) | collective-permute-done | bytes 233504 | tf_op jit(solution)/shard_map/ppermute | solution.py:137
  42.3 0.8 %collective-permute-done.10.adj_next_ref = f32[4,40,4,128]{3,2,1,0:T(4,128)S(1)} collective-permute-done((f32[4,40,4,128]{3,2,1,0:T(4,128)S(1)}, f32[4,40,4,128]{3,2,1,0:T(4,128)S(1)}, u32[]{:S(2)}, u32[]{:S(2)}) %collective-permute-start.10) | collective-permute-done | bytes 327712 | tf_op jit(solution)/shard_map/ppermute | solution.py:140
  43.1 4.6 %collective-permute-done.11.adj_prev_ref = f32[4,40,4,128]{3,2,1,0:T(4,128)S(1)} collective-permute-done((f32[4,40,4,128]{3,2,1,0:T(4,128)S(1)}, f32[4,40,4,128]{3,2,1,0:T(4,128)S(1)}, u32[]{:S(2)}, u32[]{:S(2)}) %collective-permute-start.11) | collective-permute-done | bytes 327712 | tf_op jit(solution)/shard_map/ppermute | solution.py:138
  47.7 0.0 copy-done.6
  47.7 0.0 copy-done.7
  47.7 0.0 copy-done.4
  47.7 0.7 %copy-done.5 = f32[4,40,4,128]{3,2,1,0:T(4,128)} copy-done((f32[4,40,4,128]{3,2,1,0:T(4,128)}, f32[4,40,4,128]{3,2,1,0:T(4,128)S(1)}, u32[]{:S(2)}) %copy-start.5) | copy-done | bytes 327704
  48.4 8.1 %shard_map.68 = (f32[4,32,8,128]{3,2,1,0:T(8,128)}, f32[32,8,128]{2,1,0:T(8,128)}) custom-call(s32[1]{0:T(128)} %bitcast.axis_ref, f32[4,32,8,128]{3,2,1,0:T(8,128)} %state_ref.1, f32[4,32,8,128]{3,2,1,0:T(8,128)} %adjoint_ref.1, f32[40,16,128]{2,1,0:T(8,128)} %broadcast_multiply_fusion.liner_ref, f32[4,3,8,128]{3,2,1,0:T(8,128)} %copy-done.10, ...), custom_call_target="tpu_custom_call" | custom-call | tf_op jit(solution)/shard_map/pallas_call | solution.py:154
  56.5 1.1 %slice_reduce_fusion = f32[32,8]{1,0:T(8,128)S(1)} fusion(f32[32,8,128]{2,1,0:T(8,128)} %get-tuple-element.5), kind=kLoop, calls=%fused_computation.9 | loop fusion | bytes 2048 | tf_op jit(solution)/shard_map/slice | solution.py:172
  57.6 0.1 reshape.57
  57.7 0.8 %fusion = f32[1,16,64]{2,0,1:T(1,128)S(1)} fusion(f32[256,1,1]{0,1,2:T(1,128)S(1)} %reshape.57, s32[256]{0:T(256)S(1)} %gather_fusion, s32[16,64]{1,0:T(8,128)S(1)} %multiply_add_fusion), kind=kOutput, calls=%fused_computation.1 | convolution fusion | flops 3407872 | bytes 10240 | tf_op jit(solution)/shard_map/dot_general | solution.py:177
  58.5 11.6 %all_to_all.9 = f32[32,1,64]{2,1,0:T(1,128)S(1)} all-to-all(f32[32,1,64]{2,1,0:T(1,128)S(1)} %bitcast.12), channel_id=1, replica_groups=mesh['ax'=2,'az'=16] {'ax','az'}, dimensions={0} | all-to-all | bytes 16384 | tf_op jit(solution)/shard_map/all_to_all | solution.py:180
  70.1 0.6 reduce_sum.9
  (19 shorter events, 0.1 us)
Async XLA Ops:
  0.6 0.9 %copy-start = (f32[512]{0:T(512)S(1)}, f32[512]{0:T(512)}, u32[]{:S(2)}) copy-start(f32[512]{0:T(512)} %param.7) | copy-start | bytes 6148
  0.6 15.8 %copy-start.3 = (f32[4,32,8,128]{3,2,1,0:T(8,128)S(1)}, f32[4,32,8,128]{3,2,1,0:T(8,128)}, u32[]{:S(2)}) copy-start(f32[4,32,8,128]{3,2,1,0:T(8,128)} %state_ref.1) | copy-start | bytes 1572868
  3.5 20.4 %collective-permute-start = (f32[4,8]{0,1:T(8,128)S(1)}, f32[4,8]{0,1:T(8,128)S(1)}, u32[]{:S(2)}, u32[]{:S(2)}) collective-permute-start(f32[4,8]{0,1:T(8,128)S(1)} %get-tuple-element.16), channel_id=1, source_target_pairs={{0,16},{1,17},{2,18},{3,19},{4,20},{5,21},{6,22},{7,23},{8,24},{9,... | collective-permute-start | bytes 392 | tf_op jit(solution)/shard_map/ppermute | solution.py:131
  8.4 16.8 %collective-permute-start.1 = (f32[4,8]{0,1:T(8,128)S(1)}, f32[4,8]{0,1:T(8,128)S(1)}, u32[]{:S(2)}, u32[]{:S(2)}) collective-permute-start(f32[4,8]{0,1:T(8,128)S(1)} %get-tuple-element.17), channel_id=1, source_target_pairs={{16,0},{17,1},{18,2},{19,3},{20,4},{21,5},{22,6},{23,7},{24,8},{25... | collective-permute-start | bytes 392 | tf_op jit(solution)/shard_map/ppermute | solution.py:132
  10.6 22.6 %collective-permute-start.6 = (f32[4,4,8,128]{3,2,1,0:T(8,128)S(1)}, f32[4,4,8,128]{3,2,1,0:T(8,128)S(1)}, u32[]{:S(2)}, u32[]{:S(2)}) collective-permute-start(f32[4,4,8,128]{3,2,1,0:T(8,128)S(1)} %get-tuple-element.11), channel_id=1, source_target_pairs={{0,16},{1,17},{2,18},{3,19},{4,20},{5,21},{6,22},{7,23},{8,24},{9,... | collective-permute-start | bytes 196616 | tf_op jit(solution)/shard_map/ppermute | solution.py:124
  15.2 18.7 %collective-permute-start.7 = (f32[4,4,8,128]{3,2,1,0:T(8,128)S(1)}, f32[4,4,8,128]{3,2,1,0:T(8,128)S(1)}, u32[]{:S(2)}, u32[]{:S(2)}) collective-permute-start(f32[4,4,8,128]{3,2,1,0:T(8,128)S(1)} %get-tuple-element.10), channel_id=1, source_target_pairs={{16,0},{17,1},{18,2},{19,3},{20,4},{21,5},{22,6},{23,7},{24,8},{25... | collective-permute-start | bytes 196616 | tf_op jit(solution)/shard_map/ppermute | solution.py:126
  16.5 4.6 %copy-start.12 = (s32[32,8]{0,1:T(8,128)S(1)}, s32[32,8]{0,1:T(8,128)}, u32[]{:S(2)}) copy-start(s32[32,8]{0,1:T(8,128)} %param.8) | copy-start | bytes 3076
  16.5 11.4 %collective-permute-start.4 = (f32[4,3,8,128]{3,2,1,0:T(8,128)S(1)}, f32[4,3,8,128]{3,2,1,0:T(8,128)S(1)}, u32[]{:S(2)}, u32[]{:S(2)}) collective-permute-start(f32[4,3,8,128]{3,2,1,0:T(8,128)S(1)} %get-tuple-element.13), channel_id=1, source_target_pairs={{0,16},{1,17},{2,18},{3,19},{4,20},{5,21},{6,22},{7,23},{8,24},{9,... | collective-permute-start | bytes 147464 | tf_op jit(solution)/shard_map/ppermute | solution.py:123
  21.3 0.7 copy-start.1
  23.9 6.0 %collective-permute-start.5 = (f32[4,3,8,128]{3,2,1,0:T(8,128)S(1)}, f32[4,3,8,128]{3,2,1,0:T(8,128)S(1)}, u32[]{:S(2)}, u32[]{:S(2)}) collective-permute-start(f32[4,3,8,128]{3,2,1,0:T(8,128)S(1)} %get-tuple-element.12), channel_id=1, source_target_pairs={{16,0},{17,1},{18,2},{19,3},{20,4},{21,5},{22,6},{23,7},{24,8},{25... | collective-permute-start | bytes 147464 | tf_op jit(solution)/shard_map/ppermute | solution.py:125
  25.3 13.2 %collective-permute-start.2 = (f32[40,4]{0,1:T(4,128)S(1)}, f32[40,4]{0,1:T(4,128)S(1)}, u32[]{:S(2)}, u32[]{:S(2)}) collective-permute-start(f32[40,4]{0,1:T(4,128)S(1)} %get-tuple-element.14), channel_id=1, source_target_pairs={{1,0},{2,1},{3,2},{4,3},{5,4},{6,5},{7,6},{8,7},{9,8},{10,9},{11,1... | collective-permute-start | bytes 1928 | tf_op jit(solution)/shard_map/ppermute | solution.py:142
  27.9 0.6 copy-start.10
  27.9 10.6 %collective-permute-start.3 = (f32[40,4]{0,1:T(4,128)S(1)}, f32[40,4]{0,1:T(4,128)S(1)}, u32[]{:S(2)}, u32[]{:S(2)}) collective-permute-start(f32[40,4]{0,1:T(4,128)S(1)} %get-tuple-element.15), channel_id=1, source_target_pairs={{0,1},{1,2},{2,3},{3,4},{4,5},{5,6},{6,7},{7,8},{8,9},{9,10},{10,1... | collective-permute-start | bytes 1928 | tf_op jit(solution)/shard_map/ppermute | solution.py:141
  29.9 0.6 copy-start.11
  30.5 3.3 %copy-start.2 = (f32[4,32,8,128]{3,2,1,0:T(8,128)S(1)}, f32[4,32,8,128]{3,2,1,0:T(8,128)}, u32[]{:S(2)}) copy-start(f32[4,32,8,128]{3,2,1,0:T(8,128)} %adjoint_ref.1) | copy-start | bytes 1572868
  30.6 8.9 %collective-permute-start.8 = (f32[4,38,3,128]{3,2,1,0:T(4,128)S(1)}, f32[4,38,3,128]{3,2,1,0:T(4,128)S(1)}, u32[]{:S(2)}, u32[]{:S(2)}) collective-permute-start(f32[4,38,3,128]{3,2,1,0:T(4,128)S(1)} %get-tuple-element.9), channel_id=1, source_target_pairs={{1,0},{2,1},{3,2},{4,3},{5,4},{6,5},{7,6},{8,7},{9,8},{10,9},{11,1... | collective-permute-start | bytes 700424 | tf_op jit(solution)/shard_map/ppermute | solution.py:139
  33.2 0.6 copy-start.8
  33.2 9.1 %collective-permute-start.9 = (f32[4,38,3,128]{3,2,1,0:T(4,128)S(1)}, f32[4,38,3,128]{3,2,1,0:T(4,128)S(1)}, u32[]{:S(2)}, u32[]{:S(2)}) collective-permute-start(f32[4,38,3,128]{3,2,1,0:T(4,128)S(1)} %get-tuple-element.8), channel_id=1, source_target_pairs={{0,1},{1,2},{2,3},{3,4},{4,5},{5,6},{6,7},{7,8},{8,9},{9,10},{10,1... | collective-permute-start | bytes 700424 | tf_op jit(solution)/shard_map/ppermute | solution.py:137
  33.8 0.6 copy-start.9
  34.6 8.5 %collective-permute-start.10 = (f32[4,40,4,128]{3,2,1,0:T(4,128)S(1)}, f32[4,40,4,128]{3,2,1,0:T(4,128)S(1)}, u32[]{:S(2)}, u32[]{:S(2)}) collective-permute-start(f32[4,40,4,128]{3,2,1,0:T(4,128)S(1)} %get-tuple-element.7), channel_id=1, source_target_pairs={{1,0},{2,1},{3,2},{4,3},{5,4},{6,5},{7,6},{8,7},{9,8},{10,9},{11,1... | collective-permute-start | bytes 983048 | tf_op jit(solution)/shard_map/ppermute | solution.py:140
  38.5 9.2 %collective-permute-start.11 = (f32[4,40,4,128]{3,2,1,0:T(4,128)S(1)}, f32[4,40,4,128]{3,2,1,0:T(4,128)S(1)}, u32[]{:S(2)}, u32[]{:S(2)}) collective-permute-start(f32[4,40,4,128]{3,2,1,0:T(4,128)S(1)} %get-tuple-element.6), channel_id=1, source_target_pairs={{0,1},{1,2},{2,3},{3,4},{4,5},{5,6},{6,7},{7,8},{8,9},{9,10},{10,1... | collective-permute-start | bytes 983048 | tf_op jit(solution)/shard_map/ppermute | solution.py:138
  39.5 8.1 %copy-start.6 = (f32[4,38,3,128]{3,2,1,0:T(4,128)}, f32[4,38,3,128]{3,2,1,0:T(4,128)S(1)}, u32[]{:S(2)}) copy-start(f32[4,38,3,128]{3,2,1,0:T(4,128)S(1)} %collective-permute-done.8.state_next_ref) | copy-start | bytes 700420
  42.3 5.4 %copy-start.7 = (f32[4,38,3,128]{3,2,1,0:T(4,128)}, f32[4,38,3,128]{3,2,1,0:T(4,128)S(1)}, u32[]{:S(2)}) copy-start(f32[4,38,3,128]{3,2,1,0:T(4,128)S(1)} %collective-permute-done.9.state_prev_ref) | copy-start | bytes 700420
  43.1 4.6 %copy-start.4 = (f32[4,40,4,128]{3,2,1,0:T(4,128)}, f32[4,40,4,128]{3,2,1,0:T(4,128)S(1)}, u32[]{:S(2)}) copy-start(f32[4,40,4,128]{3,2,1,0:T(4,128)S(1)} %collective-permute-done.10.adj_next_ref) | copy-start | bytes 983044
  47.7 0.7 %copy-start.5 = (f32[4,40,4,128]{3,2,1,0:T(4,128)}, f32[4,40,4,128]{3,2,1,0:T(4,128)S(1)}, u32[]{:S(2)}) copy-start(f32[4,40,4,128]{3,2,1,0:T(4,128)S(1)} %collective-permute-done.11.adj_prev_ref) | copy-start | bytes 983044

commit v4 on v2

--- a/solution.py
+++ b/solution.py
@@ -17,7 +17,7 @@
 
 def steps_kernel(
     axial_local, azim_local, radial_count, width, axial_total,
-    axis_ref, state_ref, adjoint_ref, liner_ref, axial_lo_ref, axial_hi_ref, azim_ref,
+    axis_ref, state_ref, adjoint_ref, liner_ref, axial_lo_ref, axial_hi_ref, azim_next_ref, azim_prev_ref,
     out_ref, grad_ref,
     field_a, field_b, adj_a, adj_b, liner_pad, walls, adj_walls,
 ):
@@ -26,15 +26,37 @@
     own = slice(width, width + axial_local)
     own_cols = slice(0, azim_local)
 
+    far = width - 1
+    halo_cols = slice(azim_local, cols)
+    for buf in (field_a, adj_a):
+        buf[:, 0, halo_cols] = jnp.zeros((4, 2 * width, radial_count), jnp.float32)
+        buf[:, rows - 1, halo_cols] = jnp.zeros((4, 2 * width, radial_count), jnp.float32)
+    field_a[:, :, azim_local + far : azim_local + width + 1] = jnp.zeros((4, rows, 2, radial_count), jnp.float32)
+    liner_pad[...] = jnp.zeros(liner_pad.shape, jnp.float32)
     for buf, lo in ((field_a, 0), (adj_a, 4)):
         buf[:, own, own_cols] = state_ref[...] if lo == 0 else adjoint_ref[...]
         buf[:, 0:width, own_cols] = axial_lo_ref[lo : lo + 4]
         buf[:, width + axial_local : rows, own_cols] = axial_hi_ref[lo : lo + 4]
-        buf[:, :, azim_local:cols] = azim_ref[lo : lo + 4]
+    inner = slice(1, rows - 1)
+    adj_a[:, inner, azim_local : azim_local + width] = azim_next_ref[:, :, 0:width]
+    adj_a[:, inner, azim_local + width : cols] = azim_prev_ref[:, :, 0:width]
+    field_a[:, inner, azim_local : azim_local + far] = azim_next_ref[:, :, width : width + far]
+    field_a[:, inner, cols - far : cols] = azim_prev_ref[:, :, width : width + far]
     liner_pad[own, own_cols] = liner_ref[...]
     liner_pad[0:width, own_cols] = axial_lo_ref[8]
     liner_pad[width + axial_local : rows, own_cols] = axial_hi_ref[8]
-    liner_pad[:, azim_local:cols] = azim_ref[8]
+    strip_lane = lax.broadcasted_iota(jnp.int32, (rows - 2, 1, radial_count), 2)
+    next_damp = azim_next_ref[1, :, far : far + 1, :]
+    prev_damp = azim_prev_ref[1, :, 0:1, :]
+    for m in range(far):
+        col = azim_local + m
+        liner_pad[inner, col : col + 1] = jnp.where(
+            strip_lane == radial_count - 1, pltpu.roll(next_damp, radial_count - 1 - m, 2), 0.0
+        )
+        col = cols - far + m
+        liner_pad[inner, col : col + 1] = jnp.where(
+            strip_lane == radial_count - 1, pltpu.roll(prev_damp, radial_count - 1 - m, 2), 0.0
+        )
 
     first_row = axis_ref[0] * axial_local - width
     lane = lax.broadcasted_iota(jnp.int32, (cols, radial_count), 1)
@@ -117,16 +139,28 @@
         pack(1, axial_local - width, axial_local), "ax", [(i, i + 1) for i in range(ax_count - 1)]
     ), lax.ppermute(pack(1, 0, width), "ax", [(i + 1, i) for i in range(ax_count - 1)])
 
-    def azim_pack(start, stop):
-        return jnp.concatenate(
-            [axial_lo[:, :, start:stop], pack(2, start, stop), axial_hi[:, :, start:stop]], axis=1
-        )
-
-    azim_prev = lax.ppermute(
-        azim_pack(azim_local - width, azim_local), "az", [(i, (i + 1) % az_count) for i in range(az_count)]
-    )
-    azim_next = lax.ppermute(azim_pack(0, width), "az", [((i + 1) % az_count, i) for i in range(az_count)])
-    azim_halo = jnp.concatenate([azim_next, azim_prev], axis=2)
+    far = width - 1
+
+    def padded_rows(lo, own_block, hi):
+        return jnp.concatenate([lo[:, 1:], own_block, hi[:, :-1]], axis=1)
+
+    state_rows = padded_rows(axial_lo[0:4], state, axial_hi[0:4])
+    adj_rows = padded_rows(axial_lo[4:8], final_adjoint, axial_hi[4:8])
+    damp_rows = jnp.concatenate(
+        [axial_lo[8, 1:, :, radial_count - 1], damping, axial_hi[8, :-1, :, radial_count - 1]], axis=0
+    )
+
+    def lanes(x):
+        return jnp.pad(x, ((0, 0), (0, radial_count - x.shape[1])))
+
+    next_pack = jnp.concatenate([adj_rows[:, :, 0:width], state_rows[:, :, 0:far]], axis=2)
+    next_pack = next_pack.at[1, :, far].set(lanes(damp_rows[:, 0:far]))
+    prev_pack = jnp.concatenate(
+        [adj_rows[:, :, azim_local - width :], state_rows[:, :, azim_local - far :]], axis=2
+    )
+    prev_pack = prev_pack.at[1, :, 0].set(lanes(damp_rows[:, azim_local - far :]))
+    azim_prev = lax.ppermute(prev_pack, "az", [(i, (i + 1) % az_count) for i in range(az_count)])
+    azim_next = lax.ppermute(next_pack, "az", [((i + 1) % az_count, i) for i in range(az_count)])
 
     rows = axial_local + 2 * width
     cols = azim_local + 2 * width
@@ -141,7 +175,7 @@
             jax.ShapeDtypeStruct(state.shape, jnp.float32),
             jax.ShapeDtypeStruct((axial_local, azim_local, radial_count), jnp.float32),
         ),
-        in_specs=[pl.BlockSpec(memory_space=pltpu.SMEM)] + [vmem] * 6,
+        in_specs=[pl.BlockSpec(memory_space=pltpu.SMEM)] + [vmem] * 7,
         out_specs=(vmem, vmem),
         scratch_shapes=[pltpu.VMEM((4, rows, cols, radial_count), jnp.float32)] * 4
         + [
@@ -149,7 +183,7 @@
             pltpu.VMEM((ITERS, axial_local, azim_local, radial_count), jnp.float32),
             pltpu.VMEM((ITERS, axial_local, azim_local, radial_count), jnp.float32),
         ],
-    )(axis_index, state, final_adjoint, liner, axial_lo, axial_hi, azim_halo)
+    )(axis_index, state, final_adjoint, liner, axial_lo, axial_hi, azim_next, azim_prev)
     cell_grad = grad[:, :, radial_count - 1]
 
     slot_total = 2 * resistance.shape[0]

time: 60.3 us -> 58.2 us (0.965)
  local copies, waits for them, and re-layouts: 5.43 us -> 10.8 us
  blocking collectives: 16.3 us -> 12.2 us
  waiting for transfers between devices: 14.3 us -> 12.7 us
  other arithmetic: 2.51 us -> 0.96 us
  starting transfers between devices: 9.8 us -> 9.19 us
    ppermute x2, waiting for transfers between devices: 11.5 us -> 7.22 us  [the longest x1 4.11 us: shards(): lax.ppermute(prev_pack, 'az', [(i, (i + 1) % az_count) for i in range(az_...]
    all_to_all x1, blocking collectives: 16.3 us -> 12.2 us  [shards(): patch_gradient = lax.all_to_all(send, ('ax', 'az'), 0, 0, tiled=True).sum(0)]
    unnamed x17 -> x21, local copies, waits for them, and re-layouts: 0.89 us -> 3.83 us
    ppermute x1, waiting for transfers between devices: 1.63 us -> 3.72 us  [shards(): lax.ppermute(pack(1, 0, width), 'ax', [(i + 1, i) for i in range(ax_count...]
    ppermute x0 -> x2, local copies, waits for them, and re-layouts: none -> 1.81 us  [the longest x1 0.91 us: shards(): lax.ppermute(prev_pack, 'az', [(i, (i + 1) % az_count) for i in range(az_...]
    concatenate x3, other arithmetic: 1.79 us -> 0.25 us  [the longest x1 0.12 us: shards(): jnp.concatenate([adj_rows[:, :, 0:width], state_rows[:, :, 0:far]], axis=2)]
    ppermute x2, starting transfers between devices: 3.62 us -> 2.89 us  [the longest x1 2.83 us: shards(): lax.ppermute(next_pack, 'az', [((i + 1) % az_count, i) for i in range(az_...]
  transfers between devices with their start and end apart: 4 -> 4, of which waited for: 4 -> 4; matrix products, arithmetic and copies ran while one was open for 4% -> 6% of each run, Pallas kernels for 0% -> 0%
where the time goes in v4:
time: 58.2 us; the launch traced here: 57.8 us
  waiting for transfers between devices  12.7 us (22%)
  blocking collectives  12.2 us (21%)
  local copies, waits for them, and re-layouts  10.8 us (19%)
  starting transfers between devices  9.19 us (16%)
  Pallas kernels  8.4 us (14%)
  matrix products  2.68 us (5%)
  other arithmetic  0.96 us (2%)
  between operations  0.92 us (2%)
    all_to_all x1, blocking collectives, shards(): patch_gradient = lax.all_to_all(send, ('ax', 'az'), 0, 0, tiled=True).sum(0)  12.2 us
    pallas_call x1, Pallas kernels, shards(): pl.pallas_call(kernel, out_shape=(jax.ShapeDtypeStruct(state.shape, jnp.f...  8.4 us
    ppermute x1, starting transfers between devices, shards(): lax.ppermute(pack(1, axial_local - width, axial_local), 'ax', [(i, i + 1)...  5.01 us
    ppermute x1, waiting for transfers between devices, shards(): lax.ppermute(prev_pack, 'az', [(i, (i + 1) % az_count) for i in range(az_...  4.11 us
    unnamed x21, local copies, waits for them, and re-layouts  3.83 us
    ppermute x1, waiting for transfers between devices, shards(): lax.ppermute(pack(1, 0, width), 'ax', [(i + 1, i) for i in range(ax_count...  3.72 us
    ppermute x1, waiting for transfers between devices, shards(): lax.ppermute(next_pack, 'az', [((i + 1) % az_count, i) for i in range(az_...  3.12 us
    ppermute x1, starting transfers between devices, shards(): lax.ppermute(next_pack, 'az', [((i + 1) % az_count, i) for i in range(az_...  2.83 us
  transfers between devices with their start and end apart: 4, of which 4 were waited for; matrix products, arithmetic and copies ran while one was open for 6% of the time, Pallas kernels for 0%

profile of v4, /device:TPU:0, one launch (start us, length us, event | category | flops | bytes accessed | tf_op | source)
XLA Modules:
  0.0 57.8 jit_solution(17309170442468438180)
XLA Ops:
  0.6 0.0 copy-start
  0.7 0.8 %copy.27 = s32[32,8]{1,0:T(8,128)S(1)} copy(s32[32,8]{0,1:T(8,128)} %param.12) | data formatting | bytes 2048 | tf_op args[3]
  1.4 0.0 copy-done
  1.4 1.9 %fusion.4 = f32[1,32,8]{2,0,1:T(1,128)S(1)} fusion(f32[512,1,1]{0,1,2:T(1,128)S(1)} %bitcast.15, s32[32,8]{1,0:T(8,128)S(1)} %copy.27), kind=kOutput, calls=%fused_computation.10 | convolution fusion | flops 1703936 | bytes 4096 | tf_op jit(solution)/shard_map/dot_general | solution.py:128
  3.3 0.1 broadcast_multiply_fusion.liner_ref
  3.4 0.0 copy-start.4
  3.5 1.0 %fusion.8 = (f32[4,4,8,128]{3,2,1,0:T(8,128)S(1)}, f32[4,4,8,128]{3,2,1,0:T(8,128)S(1)}, f32[4,4,8,128]{3,2,1,0:T(8,128)S(1)}, f32[4,4,8,128]{3,2,1,0:T(8,128)S(1)}) fusion(f32[4,32,8,128]{3,2,1,0:T(8,128)} %state_ref.1, f32[4,32,8,128]{3,2,1,0:T(8,128)} %adjoint_ref.1), kind=kLoop, calls=%fused_computation.32 | loop fusion | bytes 524288 | tf_op jit(solution)/shard_map/slice | solution.py:132
  4.5 0.0 copy-done.4
  4.5 0.0 copy-start.2
  4.5 5.0 %collective-permute-start = (f32[9,4,8,128]{3,2,1,0:T(8,128)S(1)}, f32[9,4,8,128]{3,2,1,0:T(8,128)S(1)}, u32[]{:S(2)}, u32[]{:S(2)}) collective-permute-start(f32[9,4,8,128]{3,2,1,0:T(8,128)S(1)} %pad_maximum_fusion.2), channel_id=1, source_target_pairs={{0,16},{1,17},{2,18},{3,19},{4,20},{5,21},{6,22},{7,23},{8,24},{9,... | collective-permute-start | bytes 442376 | tf_op jit(solution)/shard_map/ppermute | solution.py:138
  9.5 1.3 %collective-permute-start.1 = (f32[9,4,8,128]{3,2,1,0:T(8,128)S(1)}, f32[9,4,8,128]{3,2,1,0:T(8,128)S(1)}, u32[]{:S(2)}, u32[]{:S(2)}) collective-permute-start(f32[9,4,8,128]{3,2,1,0:T(8,128)S(1)} %pad_maximum_fusion.3), channel_id=1, source_target_pairs={{16,0},{17,1},{18,2},{19,3},{20,4},{21,5},{22,6},{23,7},{24,8},{25... | collective-permute-start | bytes 442376 | tf_op jit(solution)/shard_map/ppermute | solution.py:140
  10.8 1.8 %collective-permute-done.axial_lo_ref = f32[9,4,8,128]{3,2,1,0:T(8,128)S(1)} collective-permute-done((f32[9,4,8,128]{3,2,1,0:T(8,128)S(1)}, f32[9,4,8,128]{3,2,1,0:T(8,128)S(1)}, u32[]{:S(2)}, u32[]{:S(2)}) %collective-permute-start) | collective-permute-done | bytes 147488 | tf_op jit(solution)/shard_map/ppermute | solution.py:138
  12.6 0.0 copy-start.5
  12.6 0.0 copy-done.2
  12.6 0.4 copy_dynamic-update-slice_fusion
  13.0 3.7 %collective-permute-done.1.axial_hi_ref = f32[9,4,8,128]{3,2,1,0:T(8,128)S(1)} collective-permute-done((f32[9,4,8,128]{3,2,1,0:T(8,128)S(1)}, f32[9,4,8,128]{3,2,1,0:T(8,128)S(1)}, u32[]{:S(2)}, u32[]{:S(2)}) %collective-permute-start.1) | collective-permute-done | bytes 147488 | tf_op jit(solution)/shard_map/ppermute | solution.py:140
  16.7 0.0 copy-start.6
  16.8 0.0 copy-start.3
  16.9 1.0 %copy-done.3 = f32[4,32,8,128]{3,2,1,0:T(8,128)S(1)} copy-done((f32[4,32,8,128]{3,2,1,0:T(8,128)S(1)}, f32[4,32,8,128]{3,2,1,0:T(8,128)}, u32[]{:S(2)}) %copy-start.3) | copy-done | bytes 524312
  17.9 0.4 copy_dynamic-update-slice_fusion.1
  18.3 0.0 copy-done.6
  18.3 0.2 slice_reduce_fusion.1
  18.5 0.0 copy-done.5
  18.5 0.2 slice_reduce_fusion.2
  18.7 0.1 fusion.12
  18.8 0.1 pad_maximum_fusion
  18.9 0.1 scatter.6
  19.0 2.8 %collective-permute-start.2 = (f32[4,38,7,128]{3,0,2,1:T(4,128)S(1)}, f32[4,38,7,128]{3,0,2,1:T(4,128)S(1)}, u32[]{:S(2)}, u32[]{:S(2)}) collective-permute-start(f32[4,38,7,128]{3,0,2,1:T(4,128)S(1)} %scatter.6), channel_id=1, source_target_pairs={{1,0},{2,1},{3,2},{4,3},{5,4},{6,5},{7,6},{8,7},{9,8},{10,9},{11,1... | collective-permute-start | bytes 1634312 | tf_op jit(solution)/shard_map/ppermute | solution.py:163
  21.9 0.1 pad_maximum_fusion.1
  22.0 0.1 scatter.9
  22.1 0.0 copy-start.7
  22.2 0.1 collective-permute-start.3
  22.2 0.6 %copy-done.7 = s32[32,8]{0,1:T(8,128)S(1)} copy-done((s32[32,8]{0,1:T(8,128)S(1)}, s32[32,8]{0,1:T(8,128)}, u32[]{:S(2)}) %copy-start.7) | copy-done | bytes 1048
  22.8 0.1 copy.37
  22.9 0.1 reshape.129
  23.0 0.0 copy-start.1
  23.0 0.7 %copy-done.1 = s32[512]{0:T(512)S(1)} copy-done((s32[512]{0:T(512)S(1)}, s32[512]{0:T(512)}, u32[]{:S(2)}) %copy-start.1) | copy-done | bytes 2072
  23.7 1.9 %gather_fusion = s32[256]{0:T(256)S(1)} fusion(s32[512]{0:T(512)S(1)} %copy-done.1, s32[1024]{0:T(1024)S(1)} %pad_clamp_fusion), kind=kCustom, calls=%fused_computation | custom fusion | bytes 3072 | tf_op jit(solution)/shard_map/gather | solution.py:190
  25.7 3.1 %collective-permute-done.2 = f32[4,38,7,128]{3,0,2,1:T(4,128)S(1)} collective-permute-done((f32[4,38,7,128]{3,0,2,1:T(4,128)S(1)}, f32[4,38,7,128]{3,0,2,1:T(4,128)S(1)}, u32[]{:S(2)}, u32[]{:S(2)}) %collective-permute-start.2) | collective-permute-done | bytes 544800 | tf_op jit(solution)/shard_map/ppermute | solution.py:163
  28.8 0.9 %copy.35.azim_next_ref = f32[4,38,7,128]{3,2,1,0:T(8,128)} copy(f32[4,38,7,128]{3,0,2,1:T(4,128)S(1)} %collective-permute-done.2) | data formatting | bytes 1089536 | tf_op jit(solution)/shard_map/ppermute | solution.py:163
  29.7 4.1 %collective-permute-done.3 = f32[4,38,7,128]{3,0,2,1:T(4,128)S(1)} collective-permute-done((f32[4,38,7,128]{3,0,2,1:T(4,128)S(1)}, f32[4,38,7,128]{3,0,2,1:T(4,128)S(1)}, u32[]{:S(2)}, u32[]{:S(2)}) %collective-permute-start.3) | collective-permute-done | bytes 544800 | tf_op jit(solution)/shard_map/ppermute | solution.py:162
  33.8 0.9 %copy.36.azim_prev_ref = f32[4,38,7,128]{3,2,1,0:T(8,128)} copy(f32[4,38,7,128]{3,0,2,1:T(4,128)S(1)} %collective-permute-done.3) | data formatting | bytes 1089536 | tf_op jit(solution)/shard_map/ppermute | solution.py:162
  34.7 8.4 %shard_map.68 = (f32[4,32,8,128]{3,2,1,0:T(8,128)}, f32[32,8,128]{2,1,0:T(8,128)}) custom-call(s32[1]{0:T(128)} %bitcast.axis_ref, f32[4,32,8,128]{3,2,1,0:T(8,128)} %state_ref.1, f32[4,32,8,128]{3,2,1,0:T(8,128)} %adjoint_ref.1, f32[32,8,128]{2,1,0:T(8,128)} %copy-done.4, f32[9,4,8,128]{3,2,1,0:T(8,128)} %copy-done.5, f32[9,4,8,128]{3,2,1,0:T(8,128)} %copy-done.6, ...), custom_call_target="tpu_custom_call" | custom-call | tf_op jit(solution)/shard_map/pallas_call | solution.py:172
  43.1 1.1 %slice_reduce_fusion = f32[32,8]{1,0:T(8,128)S(1)} fusion(f32[32,8,128]{2,1,0:T(8,128)} %get-tuple-element.29), kind=kLoop, calls=%fused_computation.14 | loop fusion | bytes 2048 | tf_op jit(solution)/shard_map/slice | solution.py:187
  44.2 0.1 reshape.140
  44.3 0.8 %fusion = f32[1,16,64]{2,0,1:T(1,128)S(1)} fusion(f32[256,1,1]{0,1,2:T(1,128)S(1)} %reshape.140, s32[256]{0:T(256)S(1)} %gather_fusion, s32[16,64]{1,0:T(8,128)S(1)} %multiply_add_fusion), kind=kOutput, calls=%fused_computation.1 | convolution fusion | flops 3407872 | bytes 10240 | tf_op jit(solution)/shard_map/dot_general | solution.py:192
  45.1 12.2 %all_to_all.9 = f32[32,1,64]{2,1,0:T(1,128)S(1)} all-to-all(f32[32,1,64]{2,1,0:T(1,128)S(1)} %bitcast.18), channel_id=1, replica_groups=mesh['ax'=2,'az'=16] {'ax','az'}, dimensions={0} | all-to-all | bytes 16384 | tf_op jit(solution)/shard_map/all_to_all | solution.py:195
  57.3 0.6 reduce_sum.9
  (21 shorter events, 0.3 us)
Async XLA Ops:
  0.6 0.8 %copy-start = (f32[512]{0:T(512)S(1)}, f32[512]{0:T(512)}, u32[]{:S(2)}) copy-start(f32[512]{0:T(512)} %param.11) | copy-start | bytes 6148
  3.4 1.0 %copy-start.4 = (f32[32,8,128]{2,1,0:T(8,128)}, f32[32,8,128]{2,1,0:T(8,128)S(1)}, u32[]{:S(2)}) copy-start(f32[32,8,128]{2,1,0:T(8,128)S(1)} %broadcast_multiply_fusion.liner_ref) | copy-start | bytes 393220
  4.5 8.2 %copy-start.2 = (f32[4,32,8,128]{3,2,1,0:T(8,128)S(1)}, f32[4,32,8,128]{3,2,1,0:T(8,128)}, u32[]{:S(2)}) copy-start(f32[4,32,8,128]{3,2,1,0:T(8,128)} %state_ref.1) | copy-start | bytes 1572868
  4.5 8.1 %collective-permute-start = (f32[9,4,8,128]{3,2,1,0:T(8,128)S(1)}, f32[9,4,8,128]{3,2,1,0:T(8,128)S(1)}, u32[]{:S(2)}, u32[]{:S(2)}) collective-permute-start(f32[9,4,8,128]{3,2,1,0:T(8,128)S(1)} %pad_maximum_fusion.2), channel_id=1, source_target_pairs={{0,16},{1,17},{2,18},{3,19},{4,20},{5,21},{6,22},{7,23},{8,24},{9,... | collective-permute-start | bytes 442376 | tf_op jit(solution)/shard_map/ppermute | solution.py:138
  9.5 7.2 %collective-permute-start.1 = (f32[9,4,8,128]{3,2,1,0:T(8,128)S(1)}, f32[9,4,8,128]{3,2,1,0:T(8,128)S(1)}, u32[]{:S(2)}, u32[]{:S(2)}) collective-permute-start(f32[9,4,8,128]{3,2,1,0:T(8,128)S(1)} %pad_maximum_fusion.3), channel_id=1, source_target_pairs={{16,0},{17,1},{18,2},{19,3},{20,4},{21,5},{22,6},{23,7},{24,8},{25... | collective-permute-start | bytes 442376 | tf_op jit(solution)/shard_map/ppermute | solution.py:140
  12.6 5.9 %copy-start.5 = (f32[9,4,8,128]{3,2,1,0:T(8,128)}, f32[9,4,8,128]{3,2,1,0:T(8,128)S(1)}, u32[]{:S(2)}) copy-start(f32[9,4,8,128]{3,2,1,0:T(8,128)S(1)} %collective-permute-done.axial_lo_ref) | copy-start | bytes 442372
  16.7 1.6 %copy-start.6 = (f32[9,4,8,128]{3,2,1,0:T(8,128)}, f32[9,4,8,128]{3,2,1,0:T(8,128)S(1)}, u32[]{:S(2)}) copy-start(f32[9,4,8,128]{3,2,1,0:T(8,128)S(1)} %collective-permute-done.1.axial_hi_ref) | copy-start | bytes 442372
  16.8 1.1 %copy-start.3 = (f32[4,32,8,128]{3,2,1,0:T(8,128)S(1)}, f32[4,32,8,128]{3,2,1,0:T(8,128)}, u32[]{:S(2)}) copy-start(f32[4,32,8,128]{3,2,1,0:T(8,128)} %adjoint_ref.1) | copy-start | bytes 1572868
  19.0 9.8 %collective-permute-start.2 = (f32[4,38,7,128]{3,0,2,1:T(4,128)S(1)}, f32[4,38,7,128]{3,0,2,1:T(4,128)S(1)}, u32[]{:S(2)}, u32[]{:S(2)}) collective-permute-start(f32[4,38,7,128]{3,0,2,1:T(4,128)S(1)} %scatter.6), channel_id=1, source_target_pairs={{1,0},{2,1},{3,2},{4,3},{5,4},{6,5},{7,6},{8,7},{9,8},{10,9},{11,1... | collective-permute-start | bytes 1634312 | tf_op jit(solution)/shard_map/ppermute | solution.py:163
  22.1 0.7 %copy-start.7 = (s32[32,8]{0,1:T(8,128)S(1)}, s32[32,8]{0,1:T(8,128)}, u32[]{:S(2)}) copy-start(s32[32,8]{0,1:T(8,128)} %param.12) | copy-start | bytes 3076
  22.2 11.6 %collective-permute-start.3 = (f32[4,38,7,128]{3,0,2,1:T(4,128)S(1)}, f32[4,38,7,128]{3,0,2,1:T(4,128)S(1)}, u32[]{:S(2)}, u32[]{:S(2)}) collective-permute-start(f32[4,38,7,128]{3,0,2,1:T(4,128)S(1)} %scatter.9), channel_id=1, source_target_pairs={{0,1},{1,2},{2,3},{3,4},{4,5},{5,6},{6,7},{7,8},{8,9},{9,10},{10,1... | collective-permute-start | bytes 1634312 | tf_op jit(solution)/shard_map/ppermute | solution.py:162
  23.0 0.7 %copy-start.1 = (s32[512]{0:T(512)S(1)}, s32[512]{0:T(512)}, u32[]{:S(2)}) copy-start(s32[512]{0:T(512)} %param.13) | copy-start | bytes 6148

commit v5 on v4

--- a/solution.py
+++ b/solution.py
@@ -18,7 +18,8 @@
 def steps_kernel(
     axial_local, azim_local, radial_count, width, axial_total,
     axis_ref, state_ref, adjoint_ref, liner_ref, axial_lo_ref, axial_hi_ref, azim_next_ref, azim_prev_ref,
-    out_ref, grad_ref,
+    owner_ref, place_ref,
+    out_ref, send_ref,
     field_a, field_b, adj_a, adj_b, liner_pad, walls, adj_walls,
 ):
     rows = axial_local + 2 * width
@@ -110,10 +111,19 @@
             walls[step] = fwd[step % 2][0, own, own_cols]
             adj_walls[step] = adj[step % 2][0, own, own_cols]
 
-    grad = jnp.zeros(grad_ref.shape, jnp.float32)
+    grad = jnp.zeros(walls.shape[1:], jnp.float32)
     for step in range(1, ITERS + 1):
         grad = grad - time_step * adj_walls[step - 1] * walls[ITERS - step]
-    grad_ref[...] = grad
+    by_cell = grad.reshape(axial_local * azim_local, radial_count)
+    wall_lane = (lax.broadcasted_iota(jnp.int32, (8, radial_count), 1) == radial_count - 1).astype(jnp.float32)
+    cell_row = lax.dot_general(
+        wall_lane, by_cell, (((1,), (1,)), ((), ())),
+        precision=lax.Precision.HIGHEST, preferred_element_type=jnp.float32,
+    )[0:1]
+    send_ref[...] = jnp.dot(
+        owner_ref[...] * cell_row, place_ref[...],
+        precision=lax.Precision.HIGHEST, preferred_element_type=jnp.float32,
+    )
     out_ref[...] = adj[ITERS % 2][:, own, own_cols]
 
 
@@ -169,13 +179,19 @@
         steps_kernel, axial_local, azim_local, radial_count, width, axial_local * ax_count
     )
     vmem = pl.BlockSpec(memory_space=pltpu.VMEM)
-    adjoint, grad = pl.pallas_call(
+    slot_total = 2 * resistance.shape[0]
+    owned = slot_total // az_count
+    cell_slot = patch_slot_index[wall_patch].reshape(-1)
+    senders = ax_count * az_count
+    owner = (cell_slot[None, :] // owned == jnp.arange(senders, dtype=jnp.int32)[:, None] % az_count).astype(jnp.float32)
+    place = (cell_slot[:, None] % owned == jnp.arange(owned, dtype=jnp.int32)[None, :]).astype(jnp.float32)
+    adjoint, send = pl.pallas_call(
         kernel,
         out_shape=(
             jax.ShapeDtypeStruct(state.shape, jnp.float32),
-            jax.ShapeDtypeStruct((axial_local, azim_local, radial_count), jnp.float32),
+            jax.ShapeDtypeStruct((senders, owned), jnp.float32),
         ),
-        in_specs=[pl.BlockSpec(memory_space=pltpu.SMEM)] + [vmem] * 7,
+        in_specs=[pl.BlockSpec(memory_space=pltpu.SMEM)] + [vmem] * 9,
         out_specs=(vmem, vmem),
         scratch_shapes=[pltpu.VMEM((4, rows, cols, radial_count), jnp.float32)] * 4
         + [
@@ -183,15 +199,7 @@
             pltpu.VMEM((ITERS, axial_local, azim_local, radial_count), jnp.float32),
             pltpu.VMEM((ITERS, axial_local, azim_local, radial_count), jnp.float32),
         ],
-    )(axis_index, state, final_adjoint, liner, axial_lo, axial_hi, azim_next, azim_prev)
-    cell_grad = grad[:, :, radial_count - 1]
-
-    slot_total = 2 * resistance.shape[0]
-    cell_slot = patch_slot_index[wall_patch].reshape(-1)
-    onehot = (cell_slot[:, None] == jnp.arange(slot_total, dtype=jnp.int32)[None, :]).astype(jnp.float32)
-    slot_vector = jnp.dot(cell_grad.reshape(-1), onehot, precision=lax.Precision.HIGHEST)
-    owned = slot_total // az_count
-    send = jnp.tile(slot_vector.reshape(az_count, owned), (ax_count, 1))
+    )(axis_index, state, final_adjoint, liner, axial_lo, axial_hi, azim_next, azim_prev, owner, place)
     patch_gradient = lax.all_to_all(send, ("ax", "az"), 0, 0, tiled=True).sum(0)
     return (adjoint, patch_gradient)
 

time: 58.2 us -> 57.3 us (0.985)
  waiting for transfers between devices: 12.7 us -> 7.99 us
  blocking collectives: 12.2 us -> 15.1 us
  local copies, waits for them, and re-layouts: 10.8 us -> 9.03 us
  starting transfers between devices: 9.19 us -> 10.7 us
  other arithmetic: 0.96 us -> 2.42 us
  matrix products: 2.68 us -> 1.9 us
    ppermute x1, waiting for transfers between devices: 3.12 us -> 0.01 us  [shards(): lax.ppermute(next_pack, 'az', [((i + 1) % az_count, i) for i in range(az_...]
    all_to_all x1, blocking collectives: 12.2 us -> 15.1 us  [shards(): patch_gradient = lax.all_to_all(send, ('ax', 'az'), 0, 0, tiled=True).sum(0)]
    ppermute x1, waiting for transfers between devices: 1.76 us -> 0.01 us  [shards(): lax.ppermute(pack(1, axial_local - width, axial_local), 'ax', [(i, i + 1)...]
    ppermute x1, starting transfers between devices: 2.83 us -> 4.47 us  [shards(): lax.ppermute(next_pack, 'az', [((i + 1) % az_count, i) for i in range(az_...]
    convert_element_type x0 -> x2, other arithmetic: none -> 1.44 us  [the longest x1 0.75 us: shards(): (cell_slot[:, None] % owned == jnp.arange(owned, dtype=jnp.int32)[None, :...]
    ppermute x1, waiting for transfers between devices: 4.11 us -> 5.4 us  [shards(): lax.ppermute(prev_pack, 'az', [(i, (i + 1) % az_count) for i in range(az_...]
    ppermute x1, waiting for transfers between devices: 3.72 us -> 2.59 us  [shards(): lax.ppermute(pack(1, 0, width), 'ax', [(i + 1, i) for i in range(ax_count...]
    slice x1 -> x0, local copies, waits for them, and re-layouts: 1.08 us -> none  [shards(): cell_grad = grad[:, :, radial_count - 1]]
  transfers between devices with their start and end apart: 4 -> 4, of which waited for: 4 -> 2; matrix products, arithmetic and copies ran while one was open for 6% -> 9% of each run, Pallas kernels for 0% -> 0%
where the time goes in v5:
time: 57.3 us; the launch traced here: 56.9 us
  blocking collectives  15.1 us (26%)
  starting transfers between devices  10.7 us (19%)
  local copies, waits for them, and re-layouts  9.03 us (16%)
  Pallas kernels  8.82 us (15%)
  waiting for transfers between devices  7.99 us (14%)
  other arithmetic  2.42 us (4%)
  matrix products  1.9 us (3%)
  between operations  0.95 us (2%)
    all_to_all x1, blocking collectives, shards(): patch_gradient = lax.all_to_all(send, ('ax', 'az'), 0, 0, tiled=True).sum(0)  15.1 us
    pallas_call x1, Pallas kernels, shards(): pl.pallas_call(kernel, out_shape=(jax.ShapeDtypeStruct(state.shape, jnp.f...  8.82 us
    ppermute x1, waiting for transfers between devices, shards(): lax.ppermute(prev_pack, 'az', [(i, (i + 1) % az_count) for i in range(az_...  5.4 us
    ppermute x1, starting transfers between devices, shards(): lax.ppermute(pack(1, axial_local - width, axial_local), 'ax', [(i, i + 1)...  4.88 us
    ppermute x1, starting transfers between devices, shards(): lax.ppermute(next_pack, 'az', [((i + 1) % az_count, i) for i in range(az_...  4.47 us
    unnamed x21, local copies, waits for them, and re-layouts  3.23 us
    ppermute x1, waiting for transfers between devices, shards(): lax.ppermute(pack(1, 0, width), 'ax', [(i + 1, i) for i in range(ax_count...  2.59 us
    gather x1, local copies, waits for them, and re-layouts, shards(): cell_slot = patch_slot_index[wall_patch].reshape(-1)  1.94 us
  transfers between devices with their start and end apart: 4, of which 2 were waited for; matrix products, arithmetic and copies ran while one was open for 9% of the time, Pallas kernels for 0%

profile of v5, /device:TPU:0, one launch (start us, length us, event | category | flops | bytes accessed | tf_op | source)
XLA Modules:
  0.0 56.9 jit_solution(8558625194347213883)
XLA Ops:
  0.6 0.0 copy-start
  0.7 0.8 %copy.28 = s32[32,8]{1,0:T(8,128)S(1)} copy(s32[32,8]{0,1:T(8,128)} %param.12) | data formatting | bytes 2048 | tf_op args[3]
  1.4 0.0 copy-done
  1.4 1.9 %fusion = f32[1,32,8]{2,0,1:T(1,128)S(1)} fusion(f32[512,1,1]{0,1,2:T(1,128)S(1)} %bitcast.14, s32[32,8]{1,0:T(8,128)S(1)} %copy.28), kind=kOutput, calls=%fused_computation.6 | convolution fusion | flops 1703936 | bytes 4096 | tf_op jit(solution)/shard_map/dot_general | solution.py:138
  3.3 0.1 broadcast_multiply_fusion.liner_ref
  3.4 0.0 copy-start.4
  3.5 1.0 %fusion.5 = (f32[4,4,8,128]{3,2,1,0:T(8,128)S(1)}, f32[4,4,8,128]{3,2,1,0:T(8,128)S(1)}, f32[4,4,8,128]{3,2,1,0:T(8,128)S(1)}, f32[4,4,8,128]{3,2,1,0:T(8,128)S(1)}) fusion(f32[4,32,8,128]{3,2,1,0:T(8,128)} %state_ref.1, f32[4,32,8,128]{3,2,1,0:T(8,128)} %adjoint_ref.1), kind=kLoop, calls=%fused_computation.37 | loop fusion | bytes 524288 | tf_op jit(solution)/shard_map/slice | solution.py:142
  4.5 0.0 copy-done.4
  4.5 4.9 %collective-permute-start = (f32[9,4,8,128]{3,2,1,0:T(8,128)S(1)}, f32[9,4,8,128]{3,2,1,0:T(8,128)S(1)}, u32[]{:S(2)}, u32[]{:S(2)}) collective-permute-start(f32[9,4,8,128]{3,2,1,0:T(8,128)S(1)} %pad_maximum_fusion.2), channel_id=1, source_target_pairs={{0,16},{1,17},{2,18},{3,19},{4,20},{5,21},{6,22},{7,23},{8,24},{9,... | collective-permute-start | bytes 442376 | tf_op jit(solution)/shard_map/ppermute | solution.py:148
  9.4 0.0 copy-start.7
  9.4 1.3 %collective-permute-start.1 = (f32[9,4,8,128]{3,2,1,0:T(8,128)S(1)}, f32[9,4,8,128]{3,2,1,0:T(8,128)S(1)}, u32[]{:S(2)}, u32[]{:S(2)}) collective-permute-start(f32[9,4,8,128]{3,2,1,0:T(8,128)S(1)} %pad_maximum_fusion.3), channel_id=1, source_target_pairs={{16,0},{17,1},{18,2},{19,3},{20,4},{21,5},{22,6},{23,7},{24,8},{25... | collective-permute-start | bytes 442376 | tf_op jit(solution)/shard_map/ppermute | solution.py:150
  10.7 0.0 copy-done.7
  10.7 0.1 copy.36
  10.8 0.1 reshape.204
  10.9 0.0 copy-start.1
  10.9 0.7 %copy-done.1 = s32[512]{0:T(512)S(1)} copy-done((s32[512]{0:T(512)S(1)}, s32[512]{0:T(512)}, u32[]{:S(2)}) %copy-start.1) | copy-done | bytes 2072
  11.6 0.0 copy-start.3
  11.6 1.9 %gather_fusion = s32[256]{0:T(256)S(1)} fusion(s32[512]{0:T(512)S(1)} %copy-done.1, s32[1024]{0:T(1024)S(1)} %pad_clamp_fusion), kind=kCustom, calls=%fused_computation | custom fusion | bytes 3072 | tf_op jit(solution)/shard_map/gather | solution.py:184
  13.6 0.0 collective-permute-done.axial_lo_ref
  13.6 0.0 copy-start.5
  13.6 0.0 copy-done.3
  13.6 0.4 copy_dynamic-update-slice_fusion.1
  14.0 2.6 %collective-permute-done.1.axial_hi_ref = f32[9,4,8,128]{3,2,1,0:T(8,128)S(1)} collective-permute-done((f32[9,4,8,128]{3,2,1,0:T(8,128)S(1)}, f32[9,4,8,128]{3,2,1,0:T(8,128)S(1)}, u32[]{:S(2)}, u32[]{:S(2)}) %collective-permute-start.1) | collective-permute-done | bytes 147488 | tf_op jit(solution)/shard_map/ppermute | solution.py:150
  16.6 0.0 copy-start.6
  16.7 0.0 copy-start.2
  16.7 1.0 %copy-done.2 = f32[4,32,8,128]{3,2,1,0:T(8,128)S(1)} copy-done((f32[4,32,8,128]{3,2,1,0:T(8,128)S(1)}, f32[4,32,8,128]{3,2,1,0:T(8,128)}, u32[]{:S(2)}) %copy-start.2) | copy-done | bytes 524312
  17.7 0.4 copy_dynamic-update-slice_fusion
  18.2 0.0 copy-done.6
  18.2 0.2 slice_reduce_fusion
  18.4 0.0 copy-done.5
  18.4 0.2 slice_reduce_fusion.1
  18.5 0.1 fusion.9
  18.6 0.1 pad_maximum_fusion.1
  18.8 0.1 scatter.9
  18.9 0.1 collective-permute-start.3
  19.0 0.1 pad_maximum_fusion
  19.1 0.1 scatter.6
  19.3 4.5 %collective-permute-start.2 = (f32[4,38,7,128]{3,0,2,1:T(4,128)S(1)}, f32[4,38,7,128]{3,0,2,1:T(4,128)S(1)}, u32[]{:S(2)}, u32[]{:S(2)}) collective-permute-start(f32[4,38,7,128]{3,0,2,1:T(4,128)S(1)} %scatter.6), channel_id=1, source_target_pairs={{1,0},{2,1},{3,2},{4,3},{5,4},{6,5},{7,6},{8,7},{9,8},{10,9},{11,1... | collective-permute-start | bytes 1634312 | tf_op jit(solution)/shard_map/ppermute | solution.py:173
  23.7 0.7 %compare_convert_fusion.owner_ref = f32[32,256]{1,0:T(8,128)} fusion(s32[256]{0:T(256)S(1)} %get-tuple-element.47, s32[32]{0:T(128)S(1)} %and_select_fusion.1), kind=kLoop, calls=%fused_computation.17 | loop fusion | flops 16384 | bytes 33920 | tf_op jit(solution)/shard_map/convert_element_type | solution.py:186
  24.4 0.8 %fusion.2.place_ref = f32[256,64]{1,0:T(8,128)} fusion(s32[256]{0:T(256)S(1)} %get-tuple-element.46), kind=kLoop, calls=%fused_computation.11 | loop fusion | flops 32768 | bytes 66560 | tf_op jit(solution)/shard_map/convert_element_type | solution.py:187
  25.2 5.4 %collective-permute-done.3 = f32[4,38,7,128]{3,0,2,1:T(4,128)S(1)} collective-permute-done((f32[4,38,7,128]{3,0,2,1:T(4,128)S(1)}, f32[4,38,7,128]{3,0,2,1:T(4,128)S(1)}, u32[]{:S(2)}, u32[]{:S(2)}) %collective-permute-start.3) | collective-permute-done | bytes 544800 | tf_op jit(solution)/shard_map/ppermute | solution.py:172
  30.6 0.9 %copy.38.azim_prev_ref = f32[4,38,7,128]{3,2,1,0:T(8,128)} copy(f32[4,38,7,128]{3,0,2,1:T(4,128)S(1)} %collective-permute-done.3) | data formatting | bytes 1089536 | tf_op jit(solution)/shard_map/ppermute | solution.py:172
  31.5 0.0 collective-permute-done.2
  31.5 0.9 %copy.37.azim_next_ref = f32[4,38,7,128]{3,2,1,0:T(8,128)} copy(f32[4,38,7,128]{3,0,2,1:T(4,128)S(1)} %collective-permute-done.2) | data formatting | bytes 1089536 | tf_op jit(solution)/shard_map/ppermute | solution.py:173
  32.4 8.8 %shard_map.68 = (f32[4,32,8,128]{3,2,1,0:T(8,128)}, f32[32,64]{1,0:T(8,128)}) custom-call(s32[1]{0:T(128)} %bitcast.axis_ref, f32[4,32,8,128]{3,2,1,0:T(8,128)} %state_ref.1, f32[4,32,8,128]{3,2,1,0:T(8,128)} %adjoint_ref.1, f32[32,8,128]{2,1,0:T(8,128)} %copy-done.4, f32[9,4,8,128]{3,2,1,0:T(8,128)} %copy-done.5, f32[9,4,8,128]{3,2,1,0:T(8,128)} %copy-done.6, ...), custom_call_target="tpu_custom_call" | custom-call | tf_op jit(solution)/shard_map/pallas_call | solution.py:188
  41.2 15.1 %all_to_all.9 = f32[32,1,64]{2,1,0:T(1,128)S(1)} all-to-all(f32[32,1,64]{2,1,0:T(1,128)} %bitcast.17), channel_id=1, replica_groups=mesh['ax'=2,'az'=16] {'ax','az'}, dimensions={0} | all-to-all | bytes 16384 | tf_op jit(solution)/shard_map/all_to_all | solution.py:203
  56.3 0.6 reduce_sum.9
  (21 shorter events, 0.3 us)
Async XLA Ops:
  0.6 0.8 %copy-start = (f32[512]{0:T(512)S(1)}, f32[512]{0:T(512)}, u32[]{:S(2)}) copy-start(f32[512]{0:T(512)} %param.11) | copy-start | bytes 6148
  3.4 1.0 %copy-start.4 = (f32[32,8,128]{2,1,0:T(8,128)}, f32[32,8,128]{2,1,0:T(8,128)S(1)}, u32[]{:S(2)}) copy-start(f32[32,8,128]{2,1,0:T(8,128)S(1)} %broadcast_multiply_fusion.liner_ref) | copy-start | bytes 393220
  4.5 9.1 %collective-permute-start = (f32[9,4,8,128]{3,2,1,0:T(8,128)S(1)}, f32[9,4,8,128]{3,2,1,0:T(8,128)S(1)}, u32[]{:S(2)}, u32[]{:S(2)}) collective-permute-start(f32[9,4,8,128]{3,2,1,0:T(8,128)S(1)} %pad_maximum_fusion.2), channel_id=1, source_target_pairs={{0,16},{1,17},{2,18},{3,19},{4,20},{5,21},{6,22},{7,23},{8,24},{9,... | collective-permute-start | bytes 442376 | tf_op jit(solution)/shard_map/ppermute | solution.py:148
  9.4 1.3 %copy-start.7 = (s32[32,8]{0,1:T(8,128)S(1)}, s32[32,8]{0,1:T(8,128)}, u32[]{:S(2)}) copy-start(s32[32,8]{0,1:T(8,128)} %param.12) | copy-start | bytes 3076
  9.4 7.2 %collective-permute-start.1 = (f32[9,4,8,128]{3,2,1,0:T(8,128)S(1)}, f32[9,4,8,128]{3,2,1,0:T(8,128)S(1)}, u32[]{:S(2)}, u32[]{:S(2)}) collective-permute-start(f32[9,4,8,128]{3,2,1,0:T(8,128)S(1)} %pad_maximum_fusion.3), channel_id=1, source_target_pairs={{16,0},{17,1},{18,2},{19,3},{20,4},{21,5},{22,6},{23,7},{24,8},{25... | collective-permute-start | bytes 442376 | tf_op jit(solution)/shard_map/ppermute | solution.py:150
  10.9 0.7 %copy-start.1 = (s32[512]{0:T(512)S(1)}, s32[512]{0:T(512)}, u32[]{:S(2)}) copy-start(s32[512]{0:T(512)} %param.13) | copy-start | bytes 6148
  11.6 2.0 %copy-start.3 = (f32[4,32,8,128]{3,2,1,0:T(8,128)S(1)}, f32[4,32,8,128]{3,2,1,0:T(8,128)}, u32[]{:S(2)}) copy-start(f32[4,32,8,128]{3,2,1,0:T(8,128)} %adjoint_ref.1) | copy-start | bytes 1572868
  13.6 4.8 %copy-start.5 = (f32[9,4,8,128]{3,2,1,0:T(8,128)}, f32[9,4,8,128]{3,2,1,0:T(8,128)S(1)}, u32[]{:S(2)}) copy-start(f32[9,4,8,128]{3,2,1,0:T(8,128)S(1)} %collective-permute-done.axial_lo_ref) | copy-start | bytes 442372
  16.6 1.6 %copy-start.6 = (f32[9,4,8,128]{3,2,1,0:T(8,128)}, f32[9,4,8,128]{3,2,1,0:T(8,128)S(1)}, u32[]{:S(2)}) copy-start(f32[9,4,8,128]{3,2,1,0:T(8,128)S(1)} %collective-permute-done.1.axial_hi_ref) | copy-start | bytes 442372
  16.7 1.1 %copy-start.2 = (f32[4,32,8,128]{3,2,1,0:T(8,128)S(1)}, f32[4,32,8,128]{3,2,1,0:T(8,128)}, u32[]{:S(2)}) copy-start(f32[4,32,8,128]{3,2,1,0:T(8,128)} %state_ref.1) | copy-start | bytes 1572868
  18.9 11.7 %collective-permute-start.3 = (f32[4,38,7,128]{3,0,2,1:T(4,128)S(1)}, f32[4,38,7,128]{3,0,2,1:T(4,128)S(1)}, u32[]{:S(2)}, u32[]{:S(2)}) collective-permute-start(f32[4,38,7,128]{3,0,2,1:T(4,128)S(1)} %scatter.9), channel_id=1, source_target_pairs={{0,1},{1,2},{2,3},{3,4},{4,5},{5,6},{6,7},{7,8},{8,9},{9,10},{10,1... | collective-permute-start | bytes 1634312 | tf_op jit(solution)/shard_map/ppermute | solution.py:172
  19.3 12.2 %collective-permute-start.2 = (f32[4,38,7,128]{3,0,2,1:T(4,128)S(1)}, f32[4,38,7,128]{3,0,2,1:T(4,128)S(1)}, u32[]{:S(2)}, u32[]{:S(2)}) collective-permute-start(f32[4,38,7,128]{3,0,2,1:T(4,128)S(1)} %scatter.6), channel_id=1, source_target_pairs={{1,0},{2,1},{3,2},{4,3},{5,4},{6,5},{7,6},{8,7},{9,8},{10,9},{11,1... | collective-permute-start | bytes 1634312 | tf_op jit(solution)/shard_map/ppermute | solution.py:173

commit v6 on v5

--- a/solution.py
+++ b/solution.py
@@ -8,7 +8,7 @@
 from jax.sharding import PartitionSpec as P
 
 ITERS = 4
-UNROLL = 4
+UNROLL = 6
 
 
 mach_number = 0.5

time: 57.3 us -> 56.8 us (level)
  no operation moved by 1% of the time
where the time goes in v6:
time: 56.8 us; the launch traced here: 56.4 us
  blocking collectives  15.1 us (27%)
  starting transfers between devices  10.7 us (19%)
  local copies, waits for them, and re-layouts  9.03 us (16%)
  Pallas kernels  8.37 us (15%)
  waiting for transfers between devices  7.99 us (14%)
  other arithmetic  2.42 us (4%)
  matrix products  1.9 us (3%)
  between operations  0.95 us (2%)
    all_to_all x1, blocking collectives, shards(): patch_gradient = lax.all_to_all(send, ('ax', 'az'), 0, 0, tiled=True).sum(0)  15.1 us
    pallas_call x1, Pallas kernels, shards(): pl.pallas_call(kernel, out_shape=(jax.ShapeDtypeStruct(state.shape, jnp.f...  8.37 us
    ppermute x1, waiting for transfers between devices, shards(): lax.ppermute(prev_pack, 'az', [(i, (i + 1) % az_count) for i in range(az_...  5.4 us
    ppermute x1, starting transfers between devices, shards(): lax.ppermute(pack(1, axial_local - width, axial_local), 'ax', [(i, i + 1)...  4.88 us
    ppermute x1, starting transfers between devices, shards(): lax.ppermute(next_pack, 'az', [((i + 1) % az_count, i) for i in range(az_...  4.47 us
    unnamed x21, local copies, waits for them, and re-layouts  3.23 us
    ppermute x1, waiting for transfers between devices, shards(): lax.ppermute(pack(1, 0, width), 'ax', [(i + 1, i) for i in range(ax_count...  2.59 us
    gather x1, local copies, waits for them, and re-layouts, shards(): cell_slot = patch_slot_index[wall_patch].reshape(-1)  1.94 us
  transfers between devices with their start and end apart: 4, of which 2 were waited for; matrix products, arithmetic and copies ran while one was open for 9% of the time, Pallas kernels for 0%

profile of v6, /device:TPU:0, one launch (start us, length us, event | category | flops | bytes accessed | tf_op | source)
XLA Modules:
  0.0 56.4 jit_solution(9914002920080998310)
XLA Ops:
  0.6 0.0 copy-start
  0.7 0.8 %copy.28 = s32[32,8]{1,0:T(8,128)S(1)} copy(s32[32,8]{0,1:T(8,128)} %param.12) | data formatting | bytes 2048 | tf_op args[3]
  1.4 0.0 copy-done
  1.4 1.9 %fusion = f32[1,32,8]{2,0,1:T(1,128)S(1)} fusion(f32[512,1,1]{0,1,2:T(1,128)S(1)} %bitcast.14, s32[32,8]{1,0:T(8,128)S(1)} %copy.28), kind=kOutput, calls=%fused_computation.6 | convolution fusion | flops 1703936 | bytes 4096 | tf_op jit(solution)/shard_map/dot_general | solution.py:138
  3.3 0.1 broadcast_multiply_fusion.liner_ref
  3.4 0.0 copy-start.4
  3.5 1.0 %fusion.5 = (f32[4,4,8,128]{3,2,1,0:T(8,128)S(1)}, f32[4,4,8,128]{3,2,1,0:T(8,128)S(1)}, f32[4,4,8,128]{3,2,1,0:T(8,128)S(1)}, f32[4,4,8,128]{3,2,1,0:T(8,128)S(1)}) fusion(f32[4,32,8,128]{3,2,1,0:T(8,128)} %state_ref.1, f32[4,32,8,128]{3,2,1,0:T(8,128)} %adjoint_ref.1), kind=kLoop, calls=%fused_computation.37 | loop fusion | bytes 524288 | tf_op jit(solution)/shard_map/slice | solution.py:142
  4.5 0.0 copy-done.4
  4.5 4.9 %collective-permute-start = (f32[9,4,8,128]{3,2,1,0:T(8,128)S(1)}, f32[9,4,8,128]{3,2,1,0:T(8,128)S(1)}, u32[]{:S(2)}, u32[]{:S(2)}) collective-permute-start(f32[9,4,8,128]{3,2,1,0:T(8,128)S(1)} %pad_maximum_fusion.2), channel_id=1, source_target_pairs={{0,16},{1,17},{2,18},{3,19},{4,20},{5,21},{6,22},{7,23},{8,24},{9,... | collective-permute-start | bytes 442376 | tf_op jit(solution)/shard_map/ppermute | solution.py:148
  9.4 0.0 copy-start.7
  9.4 1.3 %collective-permute-start.1 = (f32[9,4,8,128]{3,2,1,0:T(8,128)S(1)}, f32[9,4,8,128]{3,2,1,0:T(8,128)S(1)}, u32[]{:S(2)}, u32[]{:S(2)}) collective-permute-start(f32[9,4,8,128]{3,2,1,0:T(8,128)S(1)} %pad_maximum_fusion.3), channel_id=1, source_target_pairs={{16,0},{17,1},{18,2},{19,3},{20,4},{21,5},{22,6},{23,7},{24,8},{25... | collective-permute-start | bytes 442376 | tf_op jit(solution)/shard_map/ppermute | solution.py:150
  10.7 0.0 copy-done.7
  10.7 0.1 copy.36
  10.8 0.1 reshape.204
  10.9 0.0 copy-start.1
  10.9 0.7 %copy-done.1 = s32[512]{0:T(512)S(1)} copy-done((s32[512]{0:T(512)S(1)}, s32[512]{0:T(512)}, u32[]{:S(2)}) %copy-start.1) | copy-done | bytes 2072
  11.6 0.0 copy-start.3
  11.6 1.9 %gather_fusion = s32[256]{0:T(256)S(1)} fusion(s32[512]{0:T(512)S(1)} %copy-done.1, s32[1024]{0:T(1024)S(1)} %pad_clamp_fusion), kind=kCustom, calls=%fused_computation | custom fusion | bytes 3072 | tf_op jit(solution)/shard_map/gather | solution.py:184
  13.6 0.0 collective-permute-done.axial_lo_ref
  13.6 0.0 copy-start.5
  13.6 0.0 copy-done.3
  13.6 0.4 copy_dynamic-update-slice_fusion.1
  14.0 2.6 %collective-permute-done.1.axial_hi_ref = f32[9,4,8,128]{3,2,1,0:T(8,128)S(1)} collective-permute-done((f32[9,4,8,128]{3,2,1,0:T(8,128)S(1)}, f32[9,4,8,128]{3,2,1,0:T(8,128)S(1)}, u32[]{:S(2)}, u32[]{:S(2)}) %collective-permute-start.1) | collective-permute-done | bytes 147488 | tf_op jit(solution)/shard_map/ppermute | solution.py:150
  16.6 0.0 copy-start.6
  16.7 0.0 copy-start.2
  16.7 1.0 %copy-done.2 = f32[4,32,8,128]{3,2,1,0:T(8,128)S(1)} copy-done((f32[4,32,8,128]{3,2,1,0:T(8,128)S(1)}, f32[4,32,8,128]{3,2,1,0:T(8,128)}, u32[]{:S(2)}) %copy-start.2) | copy-done | bytes 524312
  17.7 0.4 copy_dynamic-update-slice_fusion
  18.2 0.0 copy-done.6
  18.2 0.2 slice_reduce_fusion
  18.4 0.0 copy-done.5
  18.4 0.2 slice_reduce_fusion.1
  18.5 0.1 fusion.9
  18.6 0.1 pad_maximum_fusion.1
  18.8 0.1 scatter.9
  18.9 0.1 collective-permute-start.3
  19.0 0.1 pad_maximum_fusion
  19.1 0.1 scatter.6
  19.3 4.5 %collective-permute-start.2 = (f32[4,38,7,128]{3,0,2,1:T(4,128)S(1)}, f32[4,38,7,128]{3,0,2,1:T(4,128)S(1)}, u32[]{:S(2)}, u32[]{:S(2)}) collective-permute-start(f32[4,38,7,128]{3,0,2,1:T(4,128)S(1)} %scatter.6), channel_id=1, source_target_pairs={{1,0},{2,1},{3,2},{4,3},{5,4},{6,5},{7,6},{8,7},{9,8},{10,9},{11,1... | collective-permute-start | bytes 1634312 | tf_op jit(solution)/shard_map/ppermute | solution.py:173
  23.7 0.7 %compare_convert_fusion.owner_ref = f32[32,256]{1,0:T(8,128)} fusion(s32[256]{0:T(256)S(1)} %get-tuple-element.47, s32[32]{0:T(128)S(1)} %and_select_fusion.1), kind=kLoop, calls=%fused_computation.17 | loop fusion | flops 16384 | bytes 33920 | tf_op jit(solution)/shard_map/convert_element_type | solution.py:186
  24.4 0.8 %fusion.2.place_ref = f32[256,64]{1,0:T(8,128)} fusion(s32[256]{0:T(256)S(1)} %get-tuple-element.46), kind=kLoop, calls=%fused_computation.11 | loop fusion | flops 32768 | bytes 66560 | tf_op jit(solution)/shard_map/convert_element_type | solution.py:187
  25.2 5.4 %collective-permute-done.3 = f32[4,38,7,128]{3,0,2,1:T(4,128)S(1)} collective-permute-done((f32[4,38,7,128]{3,0,2,1:T(4,128)S(1)}, f32[4,38,7,128]{3,0,2,1:T(4,128)S(1)}, u32[]{:S(2)}, u32[]{:S(2)}) %collective-permute-start.3) | collective-permute-done | bytes 544800 | tf_op jit(solution)/shard_map/ppermute | solution.py:172
  30.6 0.9 %copy.38.azim_prev_ref = f32[4,38,7,128]{3,2,1,0:T(8,128)} copy(f32[4,38,7,128]{3,0,2,1:T(4,128)S(1)} %collective-permute-done.3) | data formatting | bytes 1089536 | tf_op jit(solution)/shard_map/ppermute | solution.py:172
  31.5 0.0 collective-permute-done.2
  31.5 0.9 %copy.37.azim_next_ref = f32[4,38,7,128]{3,2,1,0:T(8,128)} copy(f32[4,38,7,128]{3,0,2,1:T(4,128)S(1)} %collective-permute-done.2) | data formatting | bytes 1089536 | tf_op jit(solution)/shard_map/ppermute | solution.py:173
  32.4 8.4 %shard_map.68 = (f32[4,32,8,128]{3,2,1,0:T(8,128)}, f32[32,64]{1,0:T(8,128)}) custom-call(s32[1]{0:T(128)} %bitcast.axis_ref, f32[4,32,8,128]{3,2,1,0:T(8,128)} %state_ref.1, f32[4,32,8,128]{3,2,1,0:T(8,128)} %adjoint_ref.1, f32[32,8,128]{2,1,0:T(8,128)} %copy-done.4, f32[9,4,8,128]{3,2,1,0:T(8,128)} %copy-done.5, f32[9,4,8,128]{3,2,1,0:T(8,128)} %copy-done.6, ...), custom_call_target="tpu_custom_call" | custom-call | tf_op jit(solution)/shard_map/pallas_call | solution.py:188
  40.8 15.1 %all_to_all.9 = f32[32,1,64]{2,1,0:T(1,128)S(1)} all-to-all(f32[32,1,64]{2,1,0:T(1,128)} %bitcast.17), channel_id=1, replica_groups=mesh['ax'=2,'az'=16] {'ax','az'}, dimensions={0} | all-to-all | bytes 16384 | tf_op jit(solution)/shard_map/all_to_all | solution.py:203
  55.9 0.6 reduce_sum.9
  (21 shorter events, 0.3 us)
Async XLA Ops:
  0.6 0.8 %copy-start = (f32[512]{0:T(512)S(1)}, f32[512]{0:T(512)}, u32[]{:S(2)}) copy-start(f32[512]{0:T(512)} %param.11) | copy-start | bytes 6148
  3.4 1.0 %copy-start.4 = (f32[32,8,128]{2,1,0:T(8,128)}, f32[32,8,128]{2,1,0:T(8,128)S(1)}, u32[]{:S(2)}) copy-start(f32[32,8,128]{2,1,0:T(8,128)S(1)} %broadcast_multiply_fusion.liner_ref) | copy-start | bytes 393220
  4.5 9.1 %collective-permute-start = (f32[9,4,8,128]{3,2,1,0:T(8,128)S(1)}, f32[9,4,8,128]{3,2,1,0:T(8,128)S(1)}, u32[]{:S(2)}, u32[]{:S(2)}) collective-permute-start(f32[9,4,8,128]{3,2,1,0:T(8,128)S(1)} %pad_maximum_fusion.2), channel_id=1, source_target_pairs={{0,16},{1,17},{2,18},{3,19},{4,20},{5,21},{6,22},{7,23},{8,24},{9,... | collective-permute-start | bytes 442376 | tf_op jit(solution)/shard_map/ppermute | solution.py:148
  9.4 1.3 %copy-start.7 = (s32[32,8]{0,1:T(8,128)S(1)}, s32[32,8]{0,1:T(8,128)}, u32[]{:S(2)}) copy-start(s32[32,8]{0,1:T(8,128)} %param.12) | copy-start | bytes 3076
  9.4 7.2 %collective-permute-start.1 = (f32[9,4,8,128]{3,2,1,0:T(8,128)S(1)}, f32[9,4,8,128]{3,2,1,0:T(8,128)S(1)}, u32[]{:S(2)}, u32[]{:S(2)}) collective-permute-start(f32[9,4,8,128]{3,2,1,0:T(8,128)S(1)} %pad_maximum_fusion.3), channel_id=1, source_target_pairs={{16,0},{17,1},{18,2},{19,3},{20,4},{21,5},{22,6},{23,7},{24,8},{25... | collective-permute-start | bytes 442376 | tf_op jit(solution)/shard_map/ppermute | solution.py:150
  10.9 0.7 %copy-start.1 = (s32[512]{0:T(512)S(1)}, s32[512]{0:T(512)}, u32[]{:S(2)}) copy-start(s32[512]{0:T(512)} %param.13) | copy-start | bytes 6148
  11.6 2.0 %copy-start.3 = (f32[4,32,8,128]{3,2,1,0:T(8,128)S(1)}, f32[4,32,8,128]{3,2,1,0:T(8,128)}, u32[]{:S(2)}) copy-start(f32[4,32,8,128]{3,2,1,0:T(8,128)} %adjoint_ref.1) | copy-start | bytes 1572868
  13.6 4.8 %copy-start.5 = (f32[9,4,8,128]{3,2,1,0:T(8,128)}, f32[9,4,8,128]{3,2,1,0:T(8,128)S(1)}, u32[]{:S(2)}) copy-start(f32[9,4,8,128]{3,2,1,0:T(8,128)S(1)} %collective-permute-done.axial_lo_ref) | copy-start | bytes 442372
  16.6 1.6 %copy-start.6 = (f32[9,4,8,128]{3,2,1,0:T(8,128)}, f32[9,4,8,128]{3,2,1,0:T(8,128)S(1)}, u32[]{:S(2)}) copy-start(f32[9,4,8,128]{3,2,1,0:T(8,128)S(1)} %collective-permute-done.1.axial_hi_ref) | copy-start | bytes 442372
  16.7 1.1 %copy-start.2 = (f32[4,32,8,128]{3,2,1,0:T(8,128)S(1)}, f32[4,32,8,128]{3,2,1,0:T(8,128)}, u32[]{:S(2)}) copy-start(f32[4,32,8,128]{3,2,1,0:T(8,128)} %state_ref.1) | copy-start | bytes 1572868
  18.9 11.7 %collective-permute-start.3 = (f32[4,38,7,128]{3,0,2,1:T(4,128)S(1)}, f32[4,38,7,128]{3,0,2,1:T(4,128)S(1)}, u32[]{:S(2)}, u32[]{:S(2)}) collective-permute-start(f32[4,38,7,128]{3,0,2,1:T(4,128)S(1)} %scatter.9), channel_id=1, source_target_pairs={{0,1},{1,2},{2,3},{3,4},{4,5},{5,6},{6,7},{7,8},{8,9},{9,10},{10,1... | collective-permute-start | bytes 1634312 | tf_op jit(solution)/shard_map/ppermute | solution.py:172
  19.3 12.2 %collective-permute-start.2 = (f32[4,38,7,128]{3,0,2,1:T(4,128)S(1)}, f32[4,38,7,128]{3,0,2,1:T(4,128)S(1)}, u32[]{:S(2)}, u32[]{:S(2)}) collective-permute-start(f32[4,38,7,128]{3,0,2,1:T(4,128)S(1)} %scatter.6), channel_id=1, source_target_pairs={{1,0},{2,1},{3,2},{4,3},{5,4},{6,5},{7,6},{8,7},{9,8},{10,9},{11,1... | collective-permute-start | bytes 1634312 | tf_op jit(solution)/shard_map/ppermute | solution.py:173

commit v7 on v6

--- a/solution.py
+++ b/solution.py
@@ -134,8 +134,14 @@
     radial_count = state.shape[3]
     wall = (jnp.arange(radial_count) == radial_count - 1).astype(jnp.float32)
     patch_count = resistance.shape[0]
-    patch_onehot = (wall_patch[:, :, None] == jnp.arange(patch_count, dtype=jnp.int32)).astype(jnp.float32)
-    damping = jnp.dot(patch_onehot, resistance, precision=lax.Precision.HIGHEST)
+    high = lax.reduce_precision(resistance, exponent_bits=8, mantissa_bits=7)
+    rest = resistance - high
+    middle = lax.reduce_precision(rest, exponent_bits=8, mantissa_bits=7)
+    low = rest - middle
+    table = jnp.stack([high, middle, low], axis=1).astype(jnp.bfloat16)
+    patch_onehot = (wall_patch[:, :, None] == jnp.arange(patch_count, dtype=jnp.int32)).astype(jnp.bfloat16)
+    parts = jnp.dot(patch_onehot, table, preferred_element_type=jnp.float32)
+    damping = (parts[..., 0] + parts[..., 1]) + parts[..., 2]
     liner = damping[:, :, None] * wall[None, None, :]
 
     def pack(sl_axis, start, stop):

time: 56.8 us -> 55.5 us (0.977)
  local copies, waits for them, and re-layouts: 9.03 us -> 7.4 us
  matrix products: 1.9 us -> 0.75 us
  other arithmetic: 2.42 us -> 3.19 us
  waiting for transfers between devices: 7.99 us -> 8.65 us
    unnamed x21 -> x19, local copies, waits for them, and re-layouts: 3.23 us -> 1.65 us
    dot_general x1, matrix products: 1.9 us -> 0.75 us  [shards(): parts = jnp.dot(patch_onehot, table, preferred_element_type=jnp.float32)]
    another operation x0 -> x1, other arithmetic: none -> 0.75 us
    ppermute x1, waiting for transfers between devices: 2.59 us -> 3.25 us  [shards(): lax.ppermute(pack(1, 0, width), 'ax', [(i + 1, i) for i in range(ax_count...]
where the time goes in v7:
time: 55.5 us; the launch traced here: 55.1 us
  blocking collectives  15.1 us (27%)
  starting transfers between devices  10.7 us (19%)
  waiting for transfers between devices  8.65 us (16%)
  Pallas kernels  8.37 us (15%)
  local copies, waits for them, and re-layouts  7.4 us (13%)
  other arithmetic  3.19 us (6%)
  between operations  0.98 us (2%)
  matrix products  0.75 us (1%)
    all_to_all x1, blocking collectives, shards(): patch_gradient = lax.all_to_all(send, ('ax', 'az'), 0, 0, tiled=True).sum(0)  15.1 us
    pallas_call x1, Pallas kernels, shards(): pl.pallas_call(kernel, out_shape=(jax.ShapeDtypeStruct(state.shape, jnp.f...  8.37 us
    ppermute x1, waiting for transfers between devices, shards(): lax.ppermute(prev_pack, 'az', [(i, (i + 1) % az_count) for i in range(az_...  5.39 us
    ppermute x1, starting transfers between devices, shards(): lax.ppermute(pack(1, axial_local - width, axial_local), 'ax', [(i, i + 1)...  4.88 us
    ppermute x1, starting transfers between devices, shards(): lax.ppermute(next_pack, 'az', [((i + 1) % az_count, i) for i in range(az_...  4.47 us
    ppermute x1, waiting for transfers between devices, shards(): lax.ppermute(pack(1, 0, width), 'ax', [(i + 1, i) for i in range(ax_count...  3.25 us
    gather x1, local copies, waits for them, and re-layouts, shards(): cell_slot = patch_slot_index[wall_patch].reshape(-1)  1.95 us
    unnamed x19, local copies, waits for them, and re-layouts  1.65 us
  transfers between devices with their start and end apart: 4, of which 2 were waited for; matrix products, arithmetic and copies ran while one was open for 9% of the time, Pallas kernels for 0%

profile of v7, /device:TPU:0, one launch (start us, length us, event | category | flops | bytes accessed | tf_op | source)
XLA Modules:
  0.0 55.1 jit_solution(15924336227817789302)
XLA Ops:
  0.6 0.0 copy-start
  0.6 0.0 copy-start.1
  0.7 0.7 %reduce-precision_convert_fusion.1 = (bf16[512]{0:T(512)(128)(2,1)S(1)}, bf16[512]{0:T(512)(128)(2,1)S(1)}, bf16[512]{0:T(512)(128)(2,1)S(1)}) fusion(f32[512]{0:T(512)} %param.11), kind=kLoop, calls=%fused_computation.37 | loop fusion | flops 3584 | bytes 5120 | tf_op jit(solution)/shard_map/convert.5
  1.4 0.8 %copy.34 = s32[32,8]{1,0:T(8,128)S(1)} copy(s32[32,8]{0,1:T(8,128)} %param.12) | data formatting | bytes 2048 | tf_op args[3]
  2.2 0.7 %fusion = f32[32,8,3]{1,2,0:T(4,128)S(1)} fusion(s32[32,8]{1,0:T(8,128)S(1)} %copy.34, bf16[512,1]{0,1:T(2,128)(2,1)S(1)} %stack.18, bf16[512,1]{0,1:T(2,128)(2,1)S(1)} %stack.17, bf16[512,1]{0,1:T(2,128)(2,1)S(1)} %stack.16), kind=kOutput, calls=%fused_computation.6 | convolution fusion | flops 926720 | bytes 7168 | tf_op jit(solution)/shard_map/dot_general | solution.py:143
  3.0 0.1 broadcast_multiply_fusion.liner_ref
  3.1 0.0 copy-start.3
  3.1 0.0 copy-done.1
  3.1 0.9 %fusion.11 = (f32[4,4,8,128]{3,2,1,0:T(8,128)S(1)}, f32[4,4,8,128]{3,2,1,0:T(8,128)S(1)}, f32[4,4,8,128]{3,2,1,0:T(8,128)S(1)}, f32[4,4,8,128]{3,2,1,0:T(8,128)S(1)}) fusion(f32[4,32,8,128]{3,2,1,0:T(8,128)S(1)} %copy-done.1, f32[4,32,8,128]{3,2,1,0:T(8,128)} %adjoint_ref.1), kind=kLoop, calls=%fused_computation.51 | loop fusion | bytes 524288 | tf_op jit(solution)/shard_map/slice | solution.py:148
  4.1 0.0 copy-done.3
  4.1 4.9 %collective-permute-start = (f32[9,4,8,128]{3,2,1,0:T(8,128)S(1)}, f32[9,4,8,128]{3,2,1,0:T(8,128)S(1)}, u32[]{:S(2)}, u32[]{:S(2)}) collective-permute-start(f32[9,4,8,128]{3,2,1,0:T(8,128)S(1)} %pad_maximum_fusion.2), channel_id=1, source_target_pairs={{0,16},{1,17},{2,18},{3,19},{4,20},{5,21},{6,22},{7,23},{8,24},{9,... | collective-permute-start | bytes 442376 | tf_op jit(solution)/shard_map/ppermute | solution.py:154
  9.0 0.0 copy-start.6
  9.0 1.3 %collective-permute-start.1 = (f32[9,4,8,128]{3,2,1,0:T(8,128)S(1)}, f32[9,4,8,128]{3,2,1,0:T(8,128)S(1)}, u32[]{:S(2)}, u32[]{:S(2)}) collective-permute-start(f32[9,4,8,128]{3,2,1,0:T(8,128)S(1)} %pad_maximum_fusion.3), channel_id=1, source_target_pairs={{16,0},{17,1},{18,2},{19,3},{20,4},{21,5},{22,6},{23,7},{24,8},{25... | collective-permute-start | bytes 442376 | tf_op jit(solution)/shard_map/ppermute | solution.py:156
  10.3 0.0 copy-done.6
  10.3 0.1 copy.43
  10.4 0.1 reshape.205
  10.5 0.0 copy-done
  10.5 0.0 copy-start.2
  10.5 1.9 %gather_fusion = s32[256]{0:T(256)S(1)} fusion(s32[512]{0:T(512)S(1)} %copy-done, s32[1024]{0:T(1024)S(1)} %pad_clamp_fusion), kind=kCustom, calls=%fused_computation | custom fusion | bytes 3072 | tf_op jit(solution)/shard_map/gather | solution.py:190
  12.5 0.0 collective-permute-done.axial_lo_ref
  12.5 0.0 copy-start.4
  12.6 0.0 copy-done.2
  12.6 0.4 copy_dynamic-update-slice_fusion.1
  13.0 3.2 %collective-permute-done.1.axial_hi_ref = f32[9,4,8,128]{3,2,1,0:T(8,128)S(1)} collective-permute-done((f32[9,4,8,128]{3,2,1,0:T(8,128)S(1)}, f32[9,4,8,128]{3,2,1,0:T(8,128)S(1)}, u32[]{:S(2)}, u32[]{:S(2)}) %collective-permute-start.1) | collective-permute-done | bytes 147488 | tf_op jit(solution)/shard_map/ppermute | solution.py:156
  16.2 0.0 copy-start.5
  16.3 0.4 copy_dynamic-update-slice_fusion
  16.8 0.1 copy-done.5
  16.9 0.2 slice_reduce_fusion
  17.0 0.0 copy-done.4
  17.0 0.2 slice_reduce_fusion.1
  17.2 0.1 fusion.15
  17.3 0.1 pad_maximum_fusion.1
  17.4 0.1 scatter.9
  17.6 0.1 collective-permute-start.3
  17.7 0.1 pad_maximum_fusion
  17.8 0.1 scatter.6
  17.9 4.5 %collective-permute-start.2 = (f32[4,38,7,128]{3,0,2,1:T(4,128)S(1)}, f32[4,38,7,128]{3,0,2,1:T(4,128)S(1)}, u32[]{:S(2)}, u32[]{:S(2)}) collective-permute-start(f32[4,38,7,128]{3,0,2,1:T(4,128)S(1)} %scatter.6), channel_id=1, source_target_pairs={{1,0},{2,1},{3,2},{4,3},{5,4},{6,5},{7,6},{8,7},{9,8},{10,9},{11,1... | collective-permute-start | bytes 1634312 | tf_op jit(solution)/shard_map/ppermute | solution.py:179
  22.4 0.7 %compare_convert_fusion.owner_ref = f32[32,256]{1,0:T(8,128)} fusion(s32[256]{0:T(256)S(1)} %get-tuple-element.50, s32[32]{0:T(128)S(1)} %and_select_fusion.1), kind=kLoop, calls=%fused_computation.17 | loop fusion | flops 16384 | bytes 33920 | tf_op jit(solution)/shard_map/convert_element_type | solution.py:192
  23.1 0.8 %fusion.2.place_ref = f32[256,64]{1,0:T(8,128)} fusion(s32[256]{0:T(256)S(1)} %get-tuple-element.49), kind=kLoop, calls=%fused_computation.11 | loop fusion | flops 32768 | bytes 66560 | tf_op jit(solution)/shard_map/convert_element_type | solution.py:193
  23.9 5.4 %collective-permute-done.3 = f32[4,38,7,128]{3,0,2,1:T(4,128)S(1)} collective-permute-done((f32[4,38,7,128]{3,0,2,1:T(4,128)S(1)}, f32[4,38,7,128]{3,0,2,1:T(4,128)S(1)}, u32[]{:S(2)}, u32[]{:S(2)}) %collective-permute-start.3) | collective-permute-done | bytes 544800 | tf_op jit(solution)/shard_map/ppermute | solution.py:178
  29.3 0.9 %copy.45.azim_prev_ref = f32[4,38,7,128]{3,2,1,0:T(8,128)} copy(f32[4,38,7,128]{3,0,2,1:T(4,128)S(1)} %collective-permute-done.3) | data formatting | bytes 1089536 | tf_op jit(solution)/shard_map/ppermute | solution.py:178
  30.2 0.0 collective-permute-done.2
  30.2 0.9 %copy.44.azim_next_ref = f32[4,38,7,128]{3,2,1,0:T(8,128)} copy(f32[4,38,7,128]{3,0,2,1:T(4,128)S(1)} %collective-permute-done.2) | data formatting | bytes 1089536 | tf_op jit(solution)/shard_map/ppermute | solution.py:179
  31.1 8.4 %shard_map.68 = (f32[4,32,8,128]{3,2,1,0:T(8,128)}, f32[32,64]{1,0:T(8,128)}) custom-call(s32[1]{0:T(128)} %bitcast.axis_ref, f32[4,32,8,128]{3,2,1,0:T(8,128)} %state_ref.1, f32[4,32,8,128]{3,2,1,0:T(8,128)} %adjoint_ref.1, f32[32,8,128]{2,1,0:T(8,128)} %copy-done.3, f32[9,4,8,128]{3,2,1,0:T(8,128)} %copy-done.4, f32[9,4,8,128]{3,2,1,0:T(8,128)} %copy-done.5, ...), custom_call_target="tpu_custom_call" | custom-call | tf_op jit(solution)/shard_map/pallas_call | solution.py:194
  39.5 15.1 %all_to_all.9 = f32[32,1,64]{2,1,0:T(1,128)S(1)} all-to-all(f32[32,1,64]{2,1,0:T(1,128)} %bitcast.18), channel_id=1, replica_groups=mesh['ax'=2,'az'=16] {'ax','az'}, dimensions={0} | all-to-all | bytes 16384 | tf_op jit(solution)/shard_map/all_to_all | solution.py:209
  54.6 0.6 %reduce_sum.9 = f32[64]{0:T(128)} reduce(f32[32,1,64]{2,1,0:T(1,128)S(1)} %all_to_all.9, f32[]{:T(128)} %constant.110.clone.1), dimensions={0,1}, to_apply=%region_0.1 | reduce | flops 1984 | bytes 8452 | tf_op jit(solution)/shard_map/reduce_sum | solution.py:209
  (25 shorter events, 0.4 us)
Async XLA Ops:
  0.6 9.9 %copy-start = (s32[512]{0:T(512)S(1)}, s32[512]{0:T(512)}, u32[]{:S(2)}) copy-start(s32[512]{0:T(512)} %param.13) | copy-start | bytes 6148
  0.6 2.5 %copy-start.1 = (f32[4,32,8,128]{3,2,1,0:T(8,128)S(1)}, f32[4,32,8,128]{3,2,1,0:T(8,128)}, u32[]{:S(2)}) copy-start(f32[4,32,8,128]{3,2,1,0:T(8,128)} %state_ref.1) | copy-start | bytes 1572868
  3.1 1.0 %copy-start.3 = (f32[32,8,128]{2,1,0:T(8,128)}, f32[32,8,128]{2,1,0:T(8,128)S(1)}, u32[]{:S(2)}) copy-start(f32[32,8,128]{2,1,0:T(8,128)S(1)} %broadcast_multiply_fusion.liner_ref) | copy-start | bytes 393220
  4.1 8.4 %collective-permute-start = (f32[9,4,8,128]{3,2,1,0:T(8,128)S(1)}, f32[9,4,8,128]{3,2,1,0:T(8,128)S(1)}, u32[]{:S(2)}, u32[]{:S(2)}) collective-permute-start(f32[9,4,8,128]{3,2,1,0:T(8,128)S(1)} %pad_maximum_fusion.2), channel_id=1, source_target_pairs={{0,16},{1,17},{2,18},{3,19},{4,20},{5,21},{6,22},{7,23},{8,24},{9,... | collective-permute-start | bytes 442376 | tf_op jit(solution)/shard_map/ppermute | solution.py:154
  9.0 1.3 %copy-start.6 = (s32[32,8]{0,1:T(8,128)S(1)}, s32[32,8]{0,1:T(8,128)}, u32[]{:S(2)}) copy-start(s32[32,8]{0,1:T(8,128)} %param.12) | copy-start | bytes 3076
  9.0 7.2 %collective-permute-start.1 = (f32[9,4,8,128]{3,2,1,0:T(8,128)S(1)}, f32[9,4,8,128]{3,2,1,0:T(8,128)S(1)}, u32[]{:S(2)}, u32[]{:S(2)}) collective-permute-start(f32[9,4,8,128]{3,2,1,0:T(8,128)S(1)} %pad_maximum_fusion.3), channel_id=1, source_target_pairs={{16,0},{17,1},{18,2},{19,3},{20,4},{21,5},{22,6},{23,7},{24,8},{25... | collective-permute-start | bytes 442376 | tf_op jit(solution)/shard_map/ppermute | solution.py:156
  10.5 2.0 %copy-start.2 = (f32[4,32,8,128]{3,2,1,0:T(8,128)S(1)}, f32[4,32,8,128]{3,2,1,0:T(8,128)}, u32[]{:S(2)}) copy-start(f32[4,32,8,128]{3,2,1,0:T(8,128)} %adjoint_ref.1) | copy-start | bytes 1572868
  12.5 4.5 %copy-start.4 = (f32[9,4,8,128]{3,2,1,0:T(8,128)}, f32[9,4,8,128]{3,2,1,0:T(8,128)S(1)}, u32[]{:S(2)}) copy-start(f32[9,4,8,128]{3,2,1,0:T(8,128)S(1)} %collective-permute-done.axial_lo_ref) | copy-start | bytes 442372
  16.2 0.7 %copy-start.5 = (f32[9,4,8,128]{3,2,1,0:T(8,128)}, f32[9,4,8,128]{3,2,1,0:T(8,128)S(1)}, u32[]{:S(2)}) copy-start(f32[9,4,8,128]{3,2,1,0:T(8,128)S(1)} %collective-permute-done.1.axial_hi_ref) | copy-start | bytes 442372
  17.6 11.7 %collective-permute-start.3 = (f32[4,38,7,128]{3,0,2,1:T(4,128)S(1)}, f32[4,38,7,128]{3,0,2,1:T(4,128)S(1)}, u32[]{:S(2)}, u32[]{:S(2)}) collective-permute-start(f32[4,38,7,128]{3,0,2,1:T(4,128)S(1)} %scatter.9), channel_id=1, source_target_pairs={{0,1},{1,2},{2,3},{3,4},{4,5},{5,6},{6,7},{7,8},{8,9},{9,10},{10,1... | collective-permute-start | bytes 1634312 | tf_op jit(solution)/shard_map/ppermute | solution.py:178
  17.9 12.2 %collective-permute-start.2 = (f32[4,38,7,128]{3,0,2,1:T(4,128)S(1)}, f32[4,38,7,128]{3,0,2,1:T(4,128)S(1)}, u32[]{:S(2)}, u32[]{:S(2)}) collective-permute-start(f32[4,38,7,128]{3,0,2,1:T(4,128)S(1)} %scatter.6), channel_id=1, source_target_pairs={{1,0},{2,1},{3,2},{4,3},{5,4},{6,5},{7,6},{8,7},{9,8},{10,9},{11,1... | collective-permute-start | bytes 1634312 | tf_op jit(solution)/shard_map/ppermute | solution.py:179
